TPU v7x, 512 devices: a whole 4x4x16 slice. The times are simulated.
512 devices in a mesh: phase: 16 (over x, z_hi), slab: 32 (over z_lo, y, core).
Axes of the slice: x: 4, y: 4, z: 16 (z_hi: 4, z_lo: 4; z = z_hi * 4 + z_lo), core: 2. Of those that a mesh axis runs over, the one named last changes fastest.
Arguments:
- pressure: float32 [2, 64, 32, 98304], P(None, 'phase', None, 'slab'), may hold values from -6 to 6
- mode_shapes: float32 [1024, 98304], P('phase', 'slab'), may hold values from -0.0390625 to 0.0390625
- point_weight: float32 [98304], P('slab'), may hold values from 0.5 to 2
- panel_order: int32 [8], replicated, may hold values from 0 to 7, each once
Outputs:
- influence: float32 [2, 64, 32, 1024], P(None, None, 'phase', 'slab')
Inputs may be any that keep to these rules, and one draw needn't show every extreme that they name: panel_order names each of 0 to 7 once.
All inputs are finite; a program needn't handle non-finite values.
Results may differ from a plain program's by a relative error of at most 0.00007.
Values sent between devices are 32-bit elements; how exact they have to be, the bound alone decides.
No kernel may reach another device: no remote copies, remote signals or barrier semaphores. Data moves between devices by JAX's collectives and lax.ppermute only.
A program may use at most 64 MiB of HBM per device.

v0:
```python
import math

import jax
import jax.numpy as jnp
from jax import lax
from jax.sharding import PartitionSpec as P


def blade_table(blades, count):
    phases = jnp.arange(count, dtype=jnp.int32)
    target = jnp.arange(blades, dtype=jnp.int32)
    index = target[:, None] * phases[None, :] % blades
    theta = index.astype(jnp.float32) * (2.0 * math.pi / blades)
    cosine = jnp.cos(theta)
    sine = jnp.sin(theta)
    upper = jnp.concatenate([cosine, -sine], axis=1)
    lower = jnp.concatenate([sine, cosine], axis=1)
    return jnp.concatenate([upper, lower], axis=0) * (1.0 / math.sqrt(blades))


def shards(pressure, mode_shapes, point_weight, panel_order):
    weighted = mode_shapes * point_weight[None, :]
    phase_dev = pressure.shape[1]
    excite = pressure.shape[2]
    rows = pressure.reshape(2 * phase_dev * excite, pressure.shape[3])
    partial_forces = lax.dot_general(
        rows,
        lax.all_gather(weighted, "phase", axis=0, tiled=True),
        (((1,), (1,)), ((), ())),
        precision=lax.Precision.HIGHEST,
        preferred_element_type=jnp.float32,
    )
    row_count = partial_forces.shape[0]
    panel_count = panel_order.shape[0]
    panels = partial_forces.reshape(row_count, panel_count, -1)
    selector = (panel_order[:, None] == jnp.arange(panel_count, dtype=jnp.int32)[None, :]).astype(
        jnp.float32
    )
    reordered = jnp.einsum(
        "rqc,pq->rpc", panels, selector, precision=lax.Precision.HIGHEST
    ).reshape(row_count, -1)
    slab_count = lax.axis_size("slab")
    total = lax.psum(reordered, "slab")
    keep_width = total.shape[1] // slab_count
    share = lax.dynamic_slice_in_dim(total, lax.axis_index("slab") * keep_width, keep_width, 1)
    mode_local = share.shape[1]
    forces = share.reshape(2, phase_dev, excite, mode_local)
    blades = phase_dev * lax.axis_size("phase")
    gathered = lax.all_to_all(forces, "phase", split_axis=2, concat_axis=1, tiled=True)
    table = blade_table(blades, blades)
    result = jnp.dot(
        table,
        gathered.reshape(2 * blades, -1),
        precision=lax.Precision.HIGHEST,
        preferred_element_type=jnp.float32,
    )
    result = result.reshape(2, blades, -1, mode_local)
    return result


def solution(mesh):
    placed = (P(None, "phase", None, "slab"), P("phase", "slab"), P("slab"), P())
    return jax.shard_map(
        shards,
        mesh=mesh,
        in_specs=placed,
        out_specs=P(None, None, "phase", "slab"),
        check_vma=False,
    )
```

profile of v0, /device:TPU:1, one launch (start us, length us, event | category | flops | bytes accessed | tf_op | source)
XLA Modules:
  0.0 660.9 jit_solution(11755668683219762363)
XLA Ops:
  6.5 0.0 copy-start
  6.5 0.0 copy-start.1
  6.5 0.0 all-gather.2.cloned.1.call-start
  6.5 2.3 broadcast_multiply_fusion
  8.8 0.0 all-gather.2.cloned.1.call-update
  8.8 0.0 all-reduce.2.cloned.1.call-start
  8.9 308.7 %all-gather.2.cloned.1.call-done = f32[1024,3072]{1,0:T(8,128)} async-done(((f32[64,3072]{1,0:T(8,128)}), f32[1024,3072]{1,0:T(8,128)}) %all-gather.2.cloned.1.call-update) | async-done | bytes 12582928 | tf_op jit(solution)/shard_map/all_gather | solution.py:28
  317.6 0.0 copy-done
  317.6 13.5 %fusion.12 = f32[1024,256]{1,0:T(8,128)} fusion(f32[1024,3072]{1,0:T(8,128)} %all-gather.2.cloned.1.call-done, f32[256,3072]{1,0:T(8,128)S(1)} %bitcast.31), kind=kOutput, calls=%fused_computation.19 | convolution fusion | flops 9663676416 | bytes 16777216 | tf_op jit(solution)/shard_map/dot_general | solution.py:26
  331.1 2.5 copy.13
  333.6 0.0 copy-done.1
  333.6 2.9 convolution_bitcast_fusion
  336.5 2.5 copy.20
  339.1 0.0 all-reduce.2.cloned.1.call-update
  339.1 0.1 fusion.6
  339.2 285.1 %all-reduce.2.cloned.1.call-done = f32[256,1024]{0,1:T(8,128)} async-done(((f32[256,1024]{0,1:T(8,128)}), f32[256,1024]{0,1:T(8,128)}) %all-reduce.2.cloned.1.call-update) | async-done | bytes 1048592 | tf_op jit(solution)/shard_map/psum | solution.py:43
  624.4 0.8 constant_dynamic-slice_fusion
  625.1 0.1 reshape.32
  625.2 0.1 copy.15
  625.4 0.8 reshape.37
  626.1 11.7 %all-to-all-start = ((f32[16,1,512]{2,1,0:T(1,128)}), f32[16,1,512]{2,1,0:T(1,128)S(1)}, u32[]{:S(2)}, u32[]{:S(2)}) async-start(f32[16,1,512]{2,1,0:T(1,128)} %reshape.37), calls=%async_computation | async-start | bytes 65536 | tf_op jit(solution)/shard_map/all_to_all | solution.py:49
  637.8 0.1 fusion.8
  638.0 0.1 maximum_multiply_fusion
  638.1 13.4 %all-to-all-done = f32[16,1,512]{2,1,0:T(1,128)S(1)} async-done(((f32[16,1,512]{2,1,0:T(1,128)}), f32[16,1,512]{2,1,0:T(1,128)S(1)}, u32[]{:S(2)}, u32[]{:S(2)}) %all-to-all-start) | async-done | bytes 32800 | tf_op jit(solution)/shard_map/all_to_all | solution.py:49
  651.5 0.5 broadcast.24
  652.0 0.7 reduce
  652.7 0.1 reshape.38
  652.9 0.1 reshape.33
  653.1 0.1 copy.18
  653.1 1.0 fusion.13
  (2 shorter events, 0.1 us)
Async XLA Ops:
  6.5 311.1 %copy-start = (f32[2,4,32,3072]{3,2,1,0:T(8,128)S(1)}, f32[2,4,32,3072]{3,2,1,0:T(8,128)}, u32[]{:S(2)}) copy-start(f32[2,4,32,3072]{3,2,1,0:T(8,128)} %param.4) | copy-start | bytes 9437188
  6.5 327.1 %copy-start.1 = (s32[8]{0:T(128)S(1)}, s32[8]{0:T(128)}, u32[]{:S(2)}) copy-start(s32[8]{0:T(128)} %param.7) | copy-start | bytes 100
  6.5 311.1 %all-gather.2.cloned.1.call-start = ((), (), s32[]{:S(2)}) async-start(), calls=%async_computation.1 | async-start | bytes 13369344 | tf_op jit(solution)/shard_map/all_gather | solution.py:28
  8.8 615.5 %all-reduce.2.cloned.1.call-start = ((), (), s32[]{:S(2)}) async-start(), calls=%async_computation.2 | async-start | bytes 2097152 | tf_op jit(solution)/shard_map/psum | solution.py:43
  626.1 25.3 %all-to-all-start = ((f32[16,1,512]{2,1,0:T(1,128)}), f32[16,1,512]{2,1,0:T(1,128)S(1)}, u32[]{:S(2)}, u32[]{:S(2)}) async-start(f32[16,1,512]{2,1,0:T(1,128)} %reshape.37), calls=%async_computation | async-start | bytes 65536 | tf_op jit(solution)/shard_map/all_to_all | solution.py:49
Sparse Core Ops, SparseCore 0:
  10.4 307.1 all-gather.1
  339.2 285.1 all-reduce.1
where the time goes:
time: 663 us; the launch traced here: 661 us
  waiting for transfers between devices  607 us (92%)
  matrix products  17.3 us (3%)
  between operations  13.5 us (2%)
  starting transfers between devices  11.7 us (2%)
  local copies, waits for them, and re-layouts  7.73 us (1%)
    all_gather x1, waiting for transfers between devices, shards(): lax.all_gather(weighted, 'phase', axis=0, tiled=True)  309 us
    psum x1, waiting for transfers between devices, shards(): total = lax.psum(reordered, 'slab')  285 us
    dot_general x1, matrix products, shards(): lax.dot_general(rows, lax.all_gather(weighted, 'phase', axis=0, tiled=Tru...  13.5 us
    all_to_all x1, waiting for transfers between devices, shards(): lax.all_to_all(forces, 'phase', split_axis=2, concat_axis=1, tiled=True)  13.4 us
  transfers between devices with their start and end apart: 3, of which 3 were waited for; matrix products, arithmetic and copies ran while one was open for 0% of the time, Pallas kernels for 0%

commit v1 on v0

--- a/solution.py
+++ b/solution.py
@@ -39,10 +39,7 @@
     reordered = jnp.einsum(
         "rqc,pq->rpc", panels, selector, precision=lax.Precision.HIGHEST
     ).reshape(row_count, -1)
-    slab_count = lax.axis_size("slab")
-    total = lax.psum(reordered, "slab")
-    keep_width = total.shape[1] // slab_count
-    share = lax.dynamic_slice_in_dim(total, lax.axis_index("slab") * keep_width, keep_width, 1)
+    share = lax.psum_scatter(reordered, "slab", scatter_dimension=1, tiled=True)
     mode_local = share.shape[1]
     forces = share.reshape(2, phase_dev, excite, mode_local)
     blades = phase_dev * lax.axis_size("phase")

time: 663 us -> 523 us (0.79)
  waiting for transfers between devices: 607 us -> 464 us
    psum x1 -> x0, waiting for transfers between devices: 285 us -> none  [shards(): total = lax.psum(reordered, 'slab')]
    unnamed x2 -> x3, waiting for transfers between devices: 0.03 us -> 142 us
where the time goes in v1:
time: 523 us; the launch traced here: 520 us
  waiting for transfers between devices  464 us (89%)
  matrix products  17.3 us (3%)
  starting transfers between devices  13.6 us (3%)
  between operations  13.5 us (3%)
  local copies, waits for them, and re-layouts  7.67 us (1%)
    all_gather x1, waiting for transfers between devices, shards(): lax.all_gather(weighted, 'phase', axis=0, tiled=True)  309 us
    unnamed x3, waiting for transfers between devices  142 us
    all_to_all x1, starting transfers between devices, shards(): lax.all_to_all(forces, 'phase', split_axis=2, concat_axis=1, tiled=True)  13.6 us
    dot_general x1, matrix products, shards(): lax.dot_general(rows, lax.all_gather(weighted, 'phase', axis=0, tiled=Tru...  13.5 us
    all_to_all x1, waiting for transfers between devices, shards(): lax.all_to_all(forces, 'phase', split_axis=2, concat_axis=1, tiled=True)  13.4 us
  transfers between devices with their start and end apart: 3, of which 3 were waited for; matrix products, arithmetic and copies ran while one was open for 0% of the time, Pallas kernels for 0%

profile of v1, /device:TPU:1, one launch (start us, length us, event | category | flops | bytes accessed | tf_op | source)
XLA Modules:
  0.0 519.9 jit_solution(7747216759934679100)
XLA Ops:
  6.5 0.0 copy-start
  6.5 0.0 copy-start.1
  6.5 0.0 all-gather.2.cloned.1.call-start
  6.5 2.3 broadcast_multiply_fusion
  8.8 0.0 all-gather.2.cloned.1.call-update
  8.8 0.0 reduce-scatter.4.cloned.1.call-start
  8.9 308.7 %all-gather.2.cloned.1.call-done = f32[1024,3072]{1,0:T(8,128)} async-done(((f32[64,3072]{1,0:T(8,128)}), f32[1024,3072]{1,0:T(8,128)}) %all-gather.2.cloned.1.call-update) | async-done | bytes 12582928 | tf_op jit(solution)/shard_map/all_gather | solution.py:28
  317.6 0.0 copy-done
  317.6 13.5 %fusion.12 = f32[1024,256]{1,0:T(8,128)} fusion(f32[1024,3072]{1,0:T(8,128)} %all-gather.2.cloned.1.call-done, f32[256,3072]{1,0:T(8,128)S(1)} %bitcast.35), kind=kOutput, calls=%fused_computation.19 | convolution fusion | flops 9663676416 | bytes 16777216 | tf_op jit(solution)/shard_map/dot_general | solution.py:26
  331.1 2.5 copy.12
  333.6 0.0 copy-done.1
  333.6 2.9 convolution_bitcast_fusion
  336.5 2.5 copy.20
  339.1 0.0 reduce-scatter.4.cloned.1.call-update
  339.1 0.1 fusion.6
  339.2 142.3 %reduce-scatter.4.cloned.1.call-done = f32[32,256]{1,0:T(8,128)} async-done(((f32[1024,256]{1,0:T(8,128)}), f32[32,256]{1,0:T(8,128)}) %reduce-scatter.4.cloned.1.call-update) | async-done | bytes 32784
  481.5 0.9 copy.19
  482.4 0.1 copy.22
  482.5 0.8 reshape.39
  483.2 13.6 %all-to-all-start = ((f32[16,1,512]{2,1,0:T(1,128)}), f32[16,1,512]{2,1,0:T(1,128)S(1)}, u32[]{:S(2)}, u32[]{:S(2)}) async-start(f32[16,1,512]{2,1,0:T(1,128)} %reshape.39), calls=%async_computation | async-start | bytes 65536 | tf_op jit(solution)/shard_map/all_to_all | solution.py:46
  496.8 0.1 fusion.8
  496.9 0.1 maximum_multiply_fusion
  497.0 13.4 %all-to-all-done = f32[16,1,512]{2,1,0:T(1,128)S(1)} async-done(((f32[16,1,512]{2,1,0:T(1,128)}), f32[16,1,512]{2,1,0:T(1,128)S(1)}, u32[]{:S(2)}, u32[]{:S(2)}) %all-to-all-start) | async-done | bytes 32800 | tf_op jit(solution)/shard_map/all_to_all | solution.py:46
  510.5 0.5 broadcast.24
  511.0 0.7 reduce
  511.7 0.1 reshape.40
  511.9 0.1 reshape.33
  512.0 0.1 copy.16
  512.1 1.0 fusion.13
  (2 shorter events, 0.1 us)
Async XLA Ops:
  6.5 311.1 %copy-start = (f32[2,4,32,3072]{3,2,1,0:T(8,128)S(1)}, f32[2,4,32,3072]{3,2,1,0:T(8,128)}, u32[]{:S(2)}) copy-start(f32[2,4,32,3072]{3,2,1,0:T(8,128)} %param.4) | copy-start | bytes 9437188
  6.5 327.1 %copy-start.1 = (s32[8]{0:T(128)S(1)}, s32[8]{0:T(128)}, u32[]{:S(2)}) copy-start(s32[8]{0:T(128)} %param.7) | copy-start | bytes 100
  6.5 311.1 %all-gather.2.cloned.1.call-start = ((), (), s32[]{:S(2)}) async-start(), calls=%async_computation.2 | async-start | bytes 13369344 | tf_op jit(solution)/shard_map/all_gather | solution.py:28
  8.8 472.7 %reduce-scatter.4.cloned.1.call-start = ((), (), s32[]{:S(2)}) async-start(), calls=%async_computation.3 | async-start | bytes 1081344
  483.2 27.2 %all-to-all-start = ((f32[16,1,512]{2,1,0:T(1,128)}), f32[16,1,512]{2,1,0:T(1,128)S(1)}, u32[]{:S(2)}, u32[]{:S(2)}) async-start(f32[16,1,512]{2,1,0:T(1,128)} %reshape.39), calls=%async_computation | async-start | bytes 65536 | tf_op jit(solution)/shard_map/all_to_all | solution.py:46
Sparse Core Ops, SparseCore 0:
  10.4 307.1 all-gather.1
  339.2 142.2 reduce-scatter.3

commit v2 on v1

v2 whole, which is shorter than its diff:
```python
import math

import jax
import jax.numpy as jnp
from jax import lax
from jax.sharding import Mesh
from jax.sharding import PartitionSpec as P

PHASE = ("px", "pz")
SLAB = ("sz", "sy", "sc")


def blade_table(blades, count):
    phases = jnp.arange(count, dtype=jnp.int32)
    target = jnp.arange(blades, dtype=jnp.int32)
    index = target[:, None] * phases[None, :] % blades
    theta = index.astype(jnp.float32) * (2.0 * math.pi / blades)
    cosine = jnp.cos(theta)
    sine = jnp.sin(theta)
    upper = jnp.concatenate([cosine, -sine], axis=1)
    lower = jnp.concatenate([sine, cosine], axis=1)
    return jnp.concatenate([upper, lower], axis=0) * (1.0 / math.sqrt(blades))


def ring_shift(value, axis, size, shift):
    return lax.ppermute(value, axis, [(s, (s + shift) % size) for s in range(size)])


def shards(pressure, mode_shapes, point_weight, panel_order):
    nx = lax.axis_size("px")
    xi = lax.axis_index("px")
    weighted = mode_shapes * point_weight[None, :]
    column_modes = lax.all_gather(weighted, "pz", axis=0, tiled=True)
    pressure_ring = jnp.stack(
        [pressure] + [ring_shift(pressure, "px", nx, d) for d in range(1, nx)], axis=1
    )
    two, _, phase_dev, excite, points = pressure_ring.shape
    rows = pressure_ring.reshape(two * nx * phase_dev * excite, points)
    partial = lax.dot_general(
        rows,
        column_modes,
        (((1,), (1,)), ((), ())),
        precision=lax.Precision.HIGHEST,
        preferred_element_type=jnp.float32,
    )
    column_width = partial.shape[1]
    partial = partial.reshape(two, nx, phase_dev, excite, column_width)
    pieces = [partial[:, 0]] + [
        ring_shift(partial[:, d], "px", nx, -d) for d in range(1, nx)
    ]
    own = jnp.stack(pieces, axis=3)
    row_count = two * phase_dev * excite
    panel_count = panel_order.shape[0]
    local_panels = panel_count // nx
    own = own.reshape(row_count, panel_count, -1)
    slot = jnp.arange(panel_count, dtype=jnp.int32)
    stored = ((xi + slot // local_panels) % nx) * local_panels + slot % local_panels
    selector = (panel_order[:, None] == stored[None, :]).astype(jnp.float32)
    reordered = jnp.einsum(
        "rqc,pq->rpc", own, selector, precision=lax.Precision.HIGHEST
    ).reshape(row_count, -1)
    slab_count = lax.axis_size(SLAB)
    keep_width = reordered.shape[1] // slab_count
    spread = reordered.reshape(row_count, slab_count, keep_width).transpose(1, 0, 2)
    share = lax.all_to_all(spread, SLAB, 0, 0, tiled=True).sum(axis=0)
    forces = share.reshape(two, phase_dev, excite, keep_width)
    blades = phase_dev * lax.axis_size(PHASE)
    gathered = lax.all_to_all(forces, PHASE, split_axis=2, concat_axis=1, tiled=True)
    table = blade_table(blades, blades)
    result = jnp.dot(
        table,
        gathered.reshape(2 * blades, -1),
        precision=lax.Precision.HIGHEST,
        preferred_element_type=jnp.float32,
    )
    return result.reshape(2, blades, -1, keep_width)


def solution(mesh):
    phase_n, slab_n = mesh.devices.shape
    torus = Mesh(mesh.devices.reshape(4, phase_n // 4, 4, slab_n // 8, 2), PHASE + SLAB)
    placed = (P(None, PHASE, None, SLAB), P(PHASE, SLAB), P(SLAB), P())
    return jax.shard_map(
        shards,
        mesh=torus,
        in_specs=placed,
        out_specs=P(None, None, PHASE, SLAB),
        check_vma=False,
    )
```

time: 523 us -> 266 us (0.51)
  waiting for transfers between devices: 464 us -> 183 us
  starting transfers between devices: 13.6 us -> 45.2 us
    all_gather x1, waiting for transfers between devices: 309 us -> 0.01 us  [shards(): column_modes = lax.all_gather(weighted, 'pz', axis=0, tiled=True)]
    ppermute x0 -> x6, waiting for transfers between devices: none -> 143 us  [ring_shift(): lax.ppermute(value, axis, [(s, (s + shift) % size) for s in range(size)])]
    unnamed x3 -> x1, waiting for transfers between devices: 142 us -> 0.02 us
    all_to_all x1 -> x2, waiting for transfers between devices: 13.4 us -> 39.9 us  [the longest x1 26.4 us: shards(): share = lax.all_to_all(spread, SLAB, 0, 0, tiled=True).sum(axis=0)]
    ppermute x0 -> x6, starting transfers between devices: none -> 22.2 us  [ring_shift(): lax.ppermute(value, axis, [(s, (s + shift) % size) for s in range(size)])]
    all_to_all x1 -> x2, starting transfers between devices: 13.6 us -> 23 us  [the longest x1 13.5 us: shards(): lax.all_to_all(forces, PHASE, split_axis=2, concat_axis=1, tiled=True)]
  transfers between devices with their start and end apart: 3 -> 9, of which waited for: 3 -> 8; matrix products, arithmetic and copies ran while one was open for 0% -> 0% of each run, Pallas kernels for 0% -> 0%
where the time goes in v2:
time: 266 us; the launch traced here: 265 us
  waiting for transfers between devices  183 us (69%)
  starting transfers between devices  45.2 us (17%)
  matrix products  15.5 us (6%)
  between operations  13.6 us (5%)
  local copies, waits for them, and re-layouts  4.43 us (2%)
  other arithmetic  3.37 us (1%)
    ppermute x6, waiting for transfers between devices, ring_shift(): lax.ppermute(value, axis, [(s, (s + shift) % size) for s in range(size)])  143 us
    all_to_all x1, waiting for transfers between devices, shards(): share = lax.all_to_all(spread, SLAB, 0, 0, tiled=True).sum(axis=0)  26.4 us
    ppermute x6, starting transfers between devices, ring_shift(): lax.ppermute(value, axis, [(s, (s + shift) % size) for s in range(size)])  22.2 us
    dot_general x1, matrix products, shards(): lax.dot_general(rows, column_modes, (((1,), (1,)), ((), ())), precision=l...  13.9 us
    all_to_all x1, starting transfers between devices, shards(): lax.all_to_all(forces, PHASE, split_axis=2, concat_axis=1, tiled=True)  13.5 us
    all_to_all x1, waiting for transfers between devices, shards(): lax.all_to_all(forces, PHASE, split_axis=2, concat_axis=1, tiled=True)  13.4 us
    all_to_all x1, starting transfers between devices, shards(): share = lax.all_to_all(spread, SLAB, 0, 0, tiled=True).sum(axis=0)  9.53 us
  transfers between devices with their start and end apart: 9, of which 8 were waited for; matrix products, arithmetic and copies ran while one was open for 0% of the time, Pallas kernels for 0%

profile of v2, /device:TPU:1, one launch (start us, length us, event | category | flops | bytes accessed | tf_op | source)
XLA Modules:
  0.0 265.1 jit_solution(17095177698085124017)
XLA Ops:
  6.5 0.0 all-gather.2.cloned.1.call-start
  6.5 2.1 broadcast_multiply_fusion
  8.6 0.0 all-gather.2.cloned.1.call-update
  8.7 4.0 %collective-permute-start = (f32[2,4,32,3072]{3,2,1,0:T(8,128)}, f32[2,4,32,3072]{3,2,1,0:T(8,128)S(1)}, u32[]{:S(2)}, u32[]{:S(2)}) collective-permute-start(f32[2,4,32,3072]{3,2,1,0:T(8,128)} %param.4), channel_id=1, source_target_pairs={{0,128},{128,256},{256,384},{384,0},{1,129},{129,257},{257,385},{3... | collective-permute-start | bytes 9437192 | tf_op jit(solution)/shard_map/ppermute | solution.py:26
  12.6 4.4 %collective-permute-start.1 = (f32[2,4,32,3072]{3,2,1,0:T(8,128)}, f32[2,4,32,3072]{3,2,1,0:T(8,128)}, u32[]{:S(2)}, u32[]{:S(2)}) collective-permute-start(f32[2,4,32,3072]{3,2,1,0:T(8,128)} %param.4), channel_id=1, source_target_pairs={{0,256},{128,384},{256,0},{384,128},{1,257},{129,385},{257,1},{385... | collective-permute-start | bytes 9437192 | tf_op jit(solution)/shard_map/ppermute | solution.py:26
  17.0 3.1 %collective-permute-start.2 = (f32[2,4,32,3072]{3,2,1,0:T(8,128)}, f32[2,4,32,3072]{3,2,1,0:T(8,128)}, u32[]{:S(2)}, u32[]{:S(2)}) collective-permute-start(f32[2,4,32,3072]{3,2,1,0:T(8,128)} %param.4), channel_id=1, source_target_pairs={{0,384},{128,0},{256,128},{384,256},{1,385},{129,1},{257,129},{385... | collective-permute-start | bytes 9437192 | tf_op jit(solution)/shard_map/ppermute | solution.py:26
  20.1 56.0 %collective-permute-done = f32[2,4,32,3072]{3,2,1,0:T(8,128)S(1)} collective-permute-done((f32[2,4,32,3072]{3,2,1,0:T(8,128)}, f32[2,4,32,3072]{3,2,1,0:T(8,128)S(1)}, u32[]{:S(2)}, u32[]{:S(2)}) %collective-permute-start) | collective-permute-done | bytes 3145760 | tf_op jit(solution)/shard_map/ppermute | solution.py:26
  76.1 74.2 %collective-permute-done.1 = f32[2,4,32,3072]{3,2,1,0:T(8,128)} collective-permute-done((f32[2,4,32,3072]{3,2,1,0:T(8,128)}, f32[2,4,32,3072]{3,2,1,0:T(8,128)}, u32[]{:S(2)}, u32[]{:S(2)}) %collective-permute-start.1) | collective-permute-done | bytes 3145760 | tf_op jit(solution)/shard_map/ppermute | solution.py:26
  150.3 1.4 collective-permute-done.2
  151.6 0.0 all-gather.2.cloned.1.call-done
  151.6 13.9 %fusion = f32[2,4,4,32,256]{4,3,2,1,0:T(8,128)S(1)} fusion(f32[2,1,4,32,3072]{4,3,2,1,0:T(8,128)} %bitcast.7, f32[2,1,4,32,3072]{4,3,2,1,0:T(8,128)} %bitcast.6, f32[2,1,4,32,3072]{4,3,2,1,0:T(8,128)S(1)} %bitcast.63, f32[2,1,4,32,3072]{4,3,2,1,0:T(8,128)} %bitcast.62, f32[256,3072]{1,0:T(8,128)} %all-gather.2.cloned.1.call-done), kind=kOutput, calls=%fused_computation | convolution fusion | flops 9673113600 | bytes 16777216 | tf_op jit(solution)/shard_map/dot_general | solution.py:39
  165.5 0.1 slice_bitcast_fusion.3
  165.6 5.3 %collective-permute-start.3 = (f32[2,4,32,256]{3,2,1,0:T(8,128)S(1)}, f32[2,4,32,256]{3,2,1,0:T(8,128)S(1)}, u32[]{:S(2)}, u32[]{:S(2)}) collective-permute-start(f32[2,4,32,256]{3,2,1,0:T(8,128)S(1)} %get-tuple-element.6), channel_id=1, source_target_pairs={{0,384},{128,0},{256,128},{384,256},{1,385},{129,1},{257,129},{385... | collective-permute-start | bytes 786440 | tf_op jit(solution)/shard_map/ppermute | solution.py:26
  170.9 3.6 %collective-permute-start.4 = (f32[2,4,32,256]{3,2,1,0:T(8,128)S(1)}, f32[2,4,32,256]{3,2,1,0:T(8,128)S(1)}, u32[]{:S(2)}, u32[]{:S(2)}) collective-permute-start(f32[2,4,32,256]{3,2,1,0:T(8,128)S(1)} %get-tuple-element.8), channel_id=1, source_target_pairs={{0,256},{128,384},{256,0},{384,128},{1,257},{129,385},{257,1},{385... | collective-permute-start | bytes 786440 | tf_op jit(solution)/shard_map/ppermute | solution.py:26
  174.6 1.9 collective-permute-start.5
  176.5 0.6 collective-permute-done.3
  177.1 4.3 %collective-permute-done.4 = f32[2,4,32,256]{3,2,1,0:T(8,128)S(1)} collective-permute-done((f32[2,4,32,256]{3,2,1,0:T(8,128)S(1)}, f32[2,4,32,256]{3,2,1,0:T(8,128)S(1)}, u32[]{:S(2)}, u32[]{:S(2)}) %collective-permute-start.4) | collective-permute-done | bytes 262176 | tf_op jit(solution)/shard_map/ppermute | solution.py:26
  181.4 6.6 %collective-permute-done.5 = f32[2,4,32,256]{3,2,1,0:T(8,128)S(1)} collective-permute-done((f32[2,4,32,256]{3,2,1,0:T(8,128)S(1)}, f32[2,4,32,256]{3,2,1,0:T(8,128)S(1)}, u32[]{:S(2)}, u32[]{:S(2)}) %collective-permute-start.5) | collective-permute-done | bytes 262176 | tf_op jit(solution)/shard_map/ppermute | solution.py:26
  188.0 0.0 copy-start
  188.0 0.1 pad_maximum_fusion
  188.1 0.7 copy.18
  188.8 0.4 reshape.61
  189.3 0.0 copy-done
  189.3 0.6 convolution_bitcast_fusion
  189.9 1.4 copy.19
  191.3 9.5 %all-to-all-start = ((f32[32,256,32]{1,2,0:T(8,128)}), f32[32,256,32]{1,2,0:T(8,128)S(1)}, u32[]{:S(2)}, u32[]{:S(2)}) async-start(f32[32,256,32]{1,2,0:T(8,128)} %bitcast.19), calls=%async_computation | async-start | bytes 2097152 | tf_op jit(solution)/shard_map/all_to_all | solution.py:65
  200.8 0.1 fusion.15
  201.0 26.4 %all-to-all-done = f32[32,256,32]{1,2,0:T(8,128)S(1)} async-done(((f32[32,256,32]{1,2,0:T(8,128)}), f32[32,256,32]{1,2,0:T(8,128)S(1)}, u32[]{:S(2)}, u32[]{:S(2)}) %all-to-all-start) | async-done | bytes 1048608 | tf_op jit(solution)/shard_map/all_to_all | solution.py:65
  227.4 0.1 reduce_sum.9
  227.5 0.1 reshape.62
  227.6 0.1 copy.20
  227.7 0.8 reshape.68
  228.5 13.5 %all-to-all-start.1 = ((f32[16,1,512]{2,1,0:T(1,128)}), f32[16,1,512]{2,1,0:T(1,128)S(1)}, u32[]{:S(2)}, u32[]{:S(2)}) async-start(f32[16,1,512]{2,1,0:T(1,128)} %reshape.68), calls=%async_computation.1 | async-start | bytes 65536 | tf_op jit(solution)/shard_map/all_to_all | solution.py:68
  242.0 0.1 fusion.17
  242.1 0.1 maximum_multiply_fusion
  242.2 13.4 %all-to-all-done.1 = f32[16,1,512]{2,1,0:T(1,128)S(1)} async-done(((f32[16,1,512]{2,1,0:T(1,128)}), f32[16,1,512]{2,1,0:T(1,128)S(1)}, u32[]{:S(2)}, u32[]{:S(2)}) %all-to-all-start.1) | async-done | bytes 32800 | tf_op jit(solution)/shard_map/all_to_all | solution.py:68
  255.6 0.5 broadcast.109
  256.1 0.7 reduce
  256.9 0.1 reshape.69
  257.1 0.1 reshape.63
  257.2 0.1 copy.23
  257.3 1.0 fusion.27
  (3 shorter events, 0.1 us)
Async XLA Ops:
  6.5 145.1 %all-gather.2.cloned.1.call-start = ((), (), s32[]{:S(2)}) async-start(), calls=%async_computation.2 | async-start | bytes 3932160 | tf_op jit(solution)/shard_map/all_gather | solution.py:33
  8.7 67.4 %collective-permute-start = (f32[2,4,32,3072]{3,2,1,0:T(8,128)}, f32[2,4,32,3072]{3,2,1,0:T(8,128)S(1)}, u32[]{:S(2)}, u32[]{:S(2)}) collective-permute-start(f32[2,4,32,3072]{3,2,1,0:T(8,128)} %param.4), channel_id=1, source_target_pairs={{0,128},{128,256},{256,384},{384,0},{1,129},{129,257},{257,385},{3... | collective-permute-start | bytes 9437192 | tf_op jit(solution)/shard_map/ppermute | solution.py:26
  12.6 137.7 %collective-permute-start.1 = (f32[2,4,32,3072]{3,2,1,0:T(8,128)}, f32[2,4,32,3072]{3,2,1,0:T(8,128)}, u32[]{:S(2)}, u32[]{:S(2)}) collective-permute-start(f32[2,4,32,3072]{3,2,1,0:T(8,128)} %param.4), channel_id=1, source_target_pairs={{0,256},{128,384},{256,0},{384,128},{1,257},{129,385},{257,1},{385... | collective-permute-start | bytes 9437192 | tf_op jit(solution)/shard_map/ppermute | solution.py:26
  17.0 134.7 %collective-permute-start.2 = (f32[2,4,32,3072]{3,2,1,0:T(8,128)}, f32[2,4,32,3072]{3,2,1,0:T(8,128)}, u32[]{:S(2)}, u32[]{:S(2)}) collective-permute-start(f32[2,4,32,3072]{3,2,1,0:T(8,128)} %param.4), channel_id=1, source_target_pairs={{0,384},{128,0},{256,128},{384,256},{1,385},{129,1},{257,129},{385... | collective-permute-start | bytes 9437192 | tf_op jit(solution)/shard_map/ppermute | solution.py:26
  165.6 11.5 %collective-permute-start.3 = (f32[2,4,32,256]{3,2,1,0:T(8,128)S(1)}, f32[2,4,32,256]{3,2,1,0:T(8,128)S(1)}, u32[]{:S(2)}, u32[]{:S(2)}) collective-permute-start(f32[2,4,32,256]{3,2,1,0:T(8,128)S(1)} %get-tuple-element.6), channel_id=1, source_target_pairs={{0,384},{128,0},{256,128},{384,256},{1,385},{129,1},{257,129},{385... | collective-permute-start | bytes 786440 | tf_op jit(solution)/shard_map/ppermute | solution.py:26
  170.9 10.5 %collective-permute-start.4 = (f32[2,4,32,256]{3,2,1,0:T(8,128)S(1)}, f32[2,4,32,256]{3,2,1,0:T(8,128)S(1)}, u32[]{:S(2)}, u32[]{:S(2)}) collective-permute-start(f32[2,4,32,256]{3,2,1,0:T(8,128)S(1)} %get-tuple-element.8), channel_id=1, source_target_pairs={{0,256},{128,384},{256,0},{384,128},{1,257},{129,385},{257,1},{385... | collective-permute-start | bytes 786440 | tf_op jit(solution)/shard_map/ppermute | solution.py:26
  174.6 13.4 %collective-permute-start.5 = (f32[2,4,32,256]{3,2,1,0:T(8,128)S(1)}, f32[2,4,32,256]{3,2,1,0:T(8,128)S(1)}, u32[]{:S(2)}, u32[]{:S(2)}) collective-permute-start(f32[2,4,32,256]{3,2,1,0:T(8,128)S(1)} %get-tuple-element.7), channel_id=1, source_target_pairs={{0,128},{128,256},{256,384},{384,0},{1,129},{129,257},{257,385},{3... | collective-permute-start | bytes 786440 | tf_op jit(solution)/shard_map/ppermute | solution.py:26
  188.0 1.2 copy-start
  191.3 36.1 %all-to-all-start = ((f32[32,256,32]{1,2,0:T(8,128)}), f32[32,256,32]{1,2,0:T(8,128)S(1)}, u32[]{:S(2)}, u32[]{:S(2)}) async-start(f32[32,256,32]{1,2,0:T(8,128)} %bitcast.19), calls=%async_computation | async-start | bytes 2097152 | tf_op jit(solution)/shard_map/all_to_all | solution.py:65
  228.5 27.1 %all-to-all-start.1 = ((f32[16,1,512]{2,1,0:T(1,128)}), f32[16,1,512]{2,1,0:T(1,128)S(1)}, u32[]{:S(2)}, u32[]{:S(2)}) async-start(f32[16,1,512]{2,1,0:T(1,128)} %reshape.68), calls=%async_computation.1 | async-start | bytes 65536 | tf_op jit(solution)/shard_map/all_to_all | solution.py:68
Sparse Core Ops, SparseCore 0:
  9.5 134.3 all-gather.1

commit v3 on v2

--- a/solution.py
+++ b/solution.py
@@ -31,25 +31,20 @@
     xi = lax.axis_index("px")
     weighted = mode_shapes * point_weight[None, :]
     column_modes = lax.all_gather(weighted, "pz", axis=0, tiled=True)
-    pressure_ring = jnp.stack(
-        [pressure] + [ring_shift(pressure, "px", nx, d) for d in range(1, nx)], axis=1
-    )
-    two, _, phase_dev, excite, points = pressure_ring.shape
-    rows = pressure_ring.reshape(two * nx * phase_dev * excite, points)
-    partial = lax.dot_general(
-        rows,
-        column_modes,
-        (((1,), (1,)), ((), ())),
-        precision=lax.Precision.HIGHEST,
-        preferred_element_type=jnp.float32,
-    )
-    column_width = partial.shape[1]
-    partial = partial.reshape(two, nx, phase_dev, excite, column_width)
-    pieces = [partial[:, 0]] + [
-        ring_shift(partial[:, d], "px", nx, -d) for d in range(1, nx)
-    ]
-    own = jnp.stack(pieces, axis=3)
+    ring = [pressure] + [ring_shift(pressure, "px", nx, d) for d in range(1, nx)]
+    two, phase_dev, excite, points = pressure.shape
     row_count = two * phase_dev * excite
+    pieces = []
+    for d, block in enumerate(ring):
+        partial = lax.dot_general(
+            block.reshape(row_count, points),
+            column_modes,
+            (((1,), (1,)), ((), ())),
+            precision=lax.Precision.HIGHEST,
+            preferred_element_type=jnp.float32,
+        )
+        pieces.append(partial if d == 0 else ring_shift(partial, "px", nx, -d))
+    own = jnp.stack(pieces, axis=1)
     panel_count = panel_order.shape[0]
     local_panels = panel_count // nx
     own = own.reshape(row_count, panel_count, -1)
@@ -61,19 +56,25 @@
     ).reshape(row_count, -1)
     slab_count = lax.axis_size(SLAB)
     keep_width = reordered.shape[1] // slab_count
-    spread = reordered.reshape(row_count, slab_count, keep_width).transpose(1, 0, 2)
-    share = lax.all_to_all(spread, SLAB, 0, 0, tiled=True).sum(axis=0)
-    forces = share.reshape(two, phase_dev, excite, keep_width)
     blades = phase_dev * lax.axis_size(PHASE)
-    gathered = lax.all_to_all(forces, PHASE, split_axis=2, concat_axis=1, tiled=True)
     table = blade_table(blades, blades)
-    result = jnp.dot(
-        table,
-        gathered.reshape(2 * blades, -1),
-        precision=lax.Precision.HIGHEST,
-        preferred_element_type=jnp.float32,
-    )
-    return result.reshape(2, blades, -1, keep_width)
+    chains = 2
+    lane = keep_width // chains
+    spread = reordered.reshape(row_count, slab_count, chains, lane)
+    outs = []
+    for h in range(chains):
+        part = spread[:, :, h].transpose(1, 0, 2)
+        share = lax.all_to_all(part, SLAB, 0, 0, tiled=True).sum(axis=0)
+        forces = share.reshape(two, phase_dev, excite, lane)
+        gathered = lax.all_to_all(forces, PHASE, split_axis=2, concat_axis=1, tiled=True)
+        result = jnp.dot(
+            table,
+            gathered.reshape(2 * blades, -1),
+            precision=lax.Precision.HIGHEST,
+            preferred_element_type=jnp.float32,
+        )
+        outs.append(result.reshape(2, blades, -1, lane))
+    return jnp.concatenate(outs, axis=3)
 
 
 def solution(mesh):

time: 266 us -> 276 us (1.038)
  blocking collectives: 0 us -> 25 us
  waiting for transfers between devices: 183 us -> 165 us
    ppermute x6, waiting for transfers between devices: 143 us -> 61 us  [ring_shift(): lax.ppermute(value, axis, [(s, (s + shift) % size) for s in range(size)])]
    all_gather x1, waiting for transfers between devices: 0.01 us -> 65 us  [shards(): column_modes = lax.all_gather(weighted, 'pz', axis=0, tiled=True)]
    all_to_all x0 -> x1, blocking collectives: none -> 25 us  [shards(): share = lax.all_to_all(part, SLAB, 0, 0, tiled=True).sum(axis=0)]
    all_to_all x1, waiting for transfers between devices: 26.4 us -> 15.2 us  [shards(): share = lax.all_to_all(part, SLAB, 0, 0, tiled=True).sum(axis=0)]
    all_to_all x1 -> x2, waiting for transfers between devices: 13.4 us -> 24.2 us  [shards(): lax.all_to_all(forces, PHASE, split_axis=2, concat_axis=1, tiled=True)]
    all_to_all x1, starting transfers between devices: 9.53 us -> 4.15 us  [shards(): share = lax.all_to_all(part, SLAB, 0, 0, tiled=True).sum(axis=0)]
    all_to_all x1 -> x2, starting transfers between devices: 13.5 us -> 17.9 us  [shards(): lax.all_to_all(forces, PHASE, split_axis=2, concat_axis=1, tiled=True)]
    dot_general x1 -> x4, matrix products: 13.9 us -> 15.8 us  [shards(): lax.dot_general(block.reshape(row_count, points), column_modes, (((1,), (...]
  transfers between devices with their start and end apart: 9 -> 10, of which waited for: 8 -> 6; matrix products, arithmetic and copies ran while one was open for 0% -> 7% of each run, Pallas kernels for 0% -> 0%
where the time goes in v3:
time: 276 us; the launch traced here: 275 us
  waiting for transfers between devices  165 us (60%)
  starting transfers between devices  44.1 us (16%)
  blocking collectives  25 us (9%)
  matrix products  17 us (6%)
  between operations  13.7 us (5%)
  local copies, waits for them, and re-layouts  4.98 us (2%)
  other arithmetic  4.7 us (2%)
    all_gather x1, waiting for transfers between devices, shards(): column_modes = lax.all_gather(weighted, 'pz', axis=0, tiled=True)  65 us
    ppermute x6, waiting for transfers between devices, ring_shift(): lax.ppermute(value, axis, [(s, (s + shift) % size) for s in range(size)])  61 us
    all_to_all x1, blocking collectives, shards(): share = lax.all_to_all(part, SLAB, 0, 0, tiled=True).sum(axis=0)  25 us
    all_to_all x2, waiting for transfers between devices, shards(): lax.all_to_all(forces, PHASE, split_axis=2, concat_axis=1, tiled=True)  24.2 us
    ppermute x6, starting transfers between devices, ring_shift(): lax.ppermute(value, axis, [(s, (s + shift) % size) for s in range(size)])  22.1 us
    all_to_all x2, starting transfers between devices, shards(): lax.all_to_all(forces, PHASE, split_axis=2, concat_axis=1, tiled=True)  17.9 us
    dot_general x4, matrix products, shards(): lax.dot_general(block.reshape(row_count, points), column_modes, (((1,), (...  15.8 us
    all_to_all x1, waiting for transfers between devices, shards(): share = lax.all_to_all(part, SLAB, 0, 0, tiled=True).sum(axis=0)  15.2 us
  transfers between devices with their start and end apart: 10, of which 6 were waited for; matrix products, arithmetic and copies ran while one was open for 7% of the time, Pallas kernels for 0%

profile of v3, /device:TPU:1, one launch (start us, length us, event | category | flops | bytes accessed | tf_op | source)
XLA Modules:
  0.0 275.1 jit_solution(1583573060507941937)
XLA Ops:
  6.5 2.1 broadcast_multiply_fusion
  8.6 0.0 all-gather.2.cloned.1.call-update
  8.6 5.5 %collective-permute-start.2 = (f32[2,4,32,3072]{3,2,1,0:T(8,128)}, f32[2,4,32,3072]{3,2,1,0:T(8,128)}, u32[]{:S(2)}, u32[]{:S(2)}) collective-permute-start(f32[2,4,32,3072]{3,2,1,0:T(8,128)} %param.4), channel_id=1, source_target_pairs={{0,256},{128,384},{256,0},{384,128},{1,257},{129,385},{257,1},{385... | collective-permute-start | bytes 9437192 | tf_op jit(solution)/shard_map/ppermute | solution.py:26
  14.1 2.8 %collective-permute-start.4 = (f32[2,4,32,3072]{3,2,1,0:T(8,128)}, f32[2,4,32,3072]{3,2,1,0:T(8,128)}, u32[]{:S(2)}, u32[]{:S(2)}) collective-permute-start(f32[2,4,32,3072]{3,2,1,0:T(8,128)} %param.4), channel_id=1, source_target_pairs={{0,384},{128,0},{256,128},{384,256},{1,385},{129,1},{257,129},{385... | collective-permute-start | bytes 9437192 | tf_op jit(solution)/shard_map/ppermute | solution.py:26
  16.9 2.5 collective-permute-start
  19.5 59.4 %collective-permute-done.2 = f32[2,4,32,3072]{3,2,1,0:T(8,128)} collective-permute-done((f32[2,4,32,3072]{3,2,1,0:T(8,128)}, f32[2,4,32,3072]{3,2,1,0:T(8,128)}, u32[]{:S(2)}, u32[]{:S(2)}) %collective-permute-start.2) | collective-permute-done | bytes 3145760 | tf_op jit(solution)/shard_map/ppermute | solution.py:26
  78.8 65.0 %all-gather.2.cloned.1.call-done = f32[256,3072]{1,0:T(8,128)} async-done(((f32[64,3072]{1,0:T(8,128)}), f32[256,3072]{1,0:T(8,128)}) %all-gather.2.cloned.1.call-update) | async-done | bytes 3145744 | tf_op jit(solution)/shard_map/all_gather | solution.py:33
  143.8 5.7 %convolution_bitcast_fusion.2 = f32[256,256]{0,1:T(8,128)S(1)} fusion(f32[256,3072]{1,0:T(8,128)} %all-gather.2.cloned.1.call-done, f32[256,3072]{1,0:T(8,128)} %bitcast.10), kind=kOutput, calls=%fused_computation.2 | convolution fusion | flops 2415919104 | bytes 6553600 | tf_op jit(solution)/shard_map/dot_general | solution.py:39
  149.5 4.6 %collective-permute-start.3 = (f32[256,256]{0,1:T(8,128)S(1)}, f32[256,256]{0,1:T(8,128)S(1)}, u32[]{:S(2)}, u32[]{:S(2)}) collective-permute-start(f32[256,256]{0,1:T(8,128)S(1)} %convolution_bitcast_fusion.2), channel_id=1, source_target_pairs={{0,256},{128,384},{256,0},{384,128},{1,257},{129,385},{257,1},{385... | collective-permute-start | bytes 786440 | tf_op jit(solution)/shard_map/ppermute | solution.py:26
  154.1 4.6 %convolution_bitcast_fusion.1 = f32[256,256]{0,1:T(8,128)S(1)} fusion(f32[256,3072]{1,0:T(8,128)S(1)} %copy-done, f32[256,3072]{1,0:T(8,128)} %bitcast.13), kind=kOutput, calls=%fused_computation.1 | convolution fusion | flops 2415919104 | bytes 6553600 | tf_op jit(solution)/shard_map/dot_general | solution.py:39
  158.8 2.2 collective-permute-start.5
  161.0 2.7 convolution_bitcast_fusion.3
  163.7 4.5 %collective-permute-start.1 = (f32[256,256]{0,1:T(8,128)S(1)}, f32[256,256]{0,1:T(8,128)S(1)}, u32[]{:S(2)}, u32[]{:S(2)}) collective-permute-start(f32[256,256]{0,1:T(8,128)S(1)} %convolution_bitcast_fusion.3), channel_id=1, source_target_pairs={{0,384},{128,0},{256,128},{384,256},{1,385},{129,1},{257,129},{385... | collective-permute-start | bytes 786440 | tf_op jit(solution)/shard_map/ppermute | solution.py:26
  168.2 2.7 convolution_bitcast_fusion.4
  171.0 1.6 collective-permute-done.1
  172.6 0.1 pad_maximum_fusion
  172.7 0.4 copy.12
  173.1 0.6 convolution_bitcast_fusion
  173.8 0.4 copy.13
  174.2 0.9 slice_bitcast_fusion.1
  175.1 25.0 %all_to_all.40 = f32[32,256,16]{1,2,0:T(8,128)S(1)} all-to-all(f32[32,256,16]{1,2,0:T(8,128)S(1)} %get-tuple-element.5), channel_id=1, replica_groups=mesh['px'=4,'pz'=4,'sz'=4,'sy'=4,'sc'=2] {'sz','sy','sc'}, dimensions={0} | all-to-all | bytes 1048576 | tf_op jit(solution)/shard_map/all_to_all | solution.py:67
  200.1 4.1 %all-to-all-start.2 = ((f32[32,256,16]{1,2,0:T(8,128)}), f32[32,256,16]{1,2,0:T(8,128)S(1)}, u32[]{:S(2)}, u32[]{:S(2)}) async-start(f32[32,256,16]{1,2,0:T(8,128)} %get-tuple-element.6), calls=%async_computation.2 | async-start | bytes 1048576 | tf_op jit(solution)/shard_map/all_to_all | solution.py:67
  204.2 0.1 fusion.6
  204.4 0.1 reshape.89
  204.5 0.1 copy.14
  204.7 0.7 reshape.99
  205.4 15.2 %all-to-all-done.2 = f32[32,256,16]{1,2,0:T(8,128)S(1)} async-done(((f32[32,256,16]{1,2,0:T(8,128)}), f32[32,256,16]{1,2,0:T(8,128)S(1)}, u32[]{:S(2)}, u32[]{:S(2)}) %all-to-all-start.2) | async-done | bytes 524320 | tf_op jit(solution)/shard_map/all_to_all | solution.py:67
  220.6 14.4 %all-to-all-start.1 = ((f32[16,1,256]{2,1,0:T(1,128)}), f32[16,1,256]{2,1,0:T(1,128)S(1)}, u32[]{:S(2)}, u32[]{:S(2)}) async-start(f32[16,1,256]{2,1,0:T(1,128)} %reshape.99), calls=%async_computation.1 | async-start | bytes 32768 | tf_op jit(solution)/shard_map/all_to_all | solution.py:69
  235.1 0.1 fusion.8
  235.3 0.1 reshape.91
  235.4 0.1 copy.18
  235.5 0.7 reshape.97
  236.3 12.5 %all-to-all-done.1 = f32[16,1,256]{2,1,0:T(1,128)S(1)} async-done(((f32[16,1,256]{2,1,0:T(1,128)}), f32[16,1,256]{2,1,0:T(1,128)S(1)}, u32[]{:S(2)}, u32[]{:S(2)}) %all-to-all-start.1) | async-done | bytes 16416 | tf_op jit(solution)/shard_map/all_to_all | solution.py:69
  248.7 3.5 %all-to-all-start.3 = ((f32[16,1,256]{2,1,0:T(1,128)}), f32[16,1,256]{2,1,0:T(1,128)S(1)}, u32[]{:S(2)}, u32[]{:S(2)}) async-start(f32[16,1,256]{2,1,0:T(1,128)} %reshape.97), calls=%async_computation.3 | async-start | bytes 32768 | tf_op jit(solution)/shard_map/all_to_all | solution.py:69
  252.2 0.1 maximum_multiply_fusion
  252.3 0.6 broadcast.114
  252.9 0.7 reduce.1
  253.6 0.1 reshape.100
  253.9 0.1 reshape.90
  254.0 0.1 copy.17
  254.0 11.8 %all-to-all-done.3 = f32[16,1,256]{2,1,0:T(1,128)S(1)} async-done(((f32[16,1,256]{2,1,0:T(1,128)}), f32[16,1,256]{2,1,0:T(1,128)S(1)}, u32[]{:S(2)}, u32[]{:S(2)}) %all-to-all-start.3) | async-done | bytes 16416 | tf_op jit(solution)/shard_map/all_to_all | solution.py:69
  265.8 0.7 reduce
  266.5 0.1 reshape.98
  266.8 0.1 reshape.92
  266.9 0.1 copy.21
  267.0 0.3 fusion.17
  267.3 0.3 fusion.18
  267.6 0.6 pad_maximum_fusion.1
  (18 shorter events, 0.3 us)
Async XLA Ops:
  6.5 137.3 %all-gather.2.cloned.1.call-start = ((), (), s32[]{:S(2)}) async-start(), calls=%async_computation.4 | async-start | bytes 3932160 | tf_op jit(solution)/shard_map/all_gather | solution.py:33
  8.6 70.2 %collective-permute-start.2 = (f32[2,4,32,3072]{3,2,1,0:T(8,128)}, f32[2,4,32,3072]{3,2,1,0:T(8,128)}, u32[]{:S(2)}, u32[]{:S(2)}) collective-permute-start(f32[2,4,32,3072]{3,2,1,0:T(8,128)} %param.4), channel_id=1, source_target_pairs={{0,256},{128,384},{256,0},{384,128},{1,257},{129,385},{257,1},{385... | collective-permute-start | bytes 9437192 | tf_op jit(solution)/shard_map/ppermute | solution.py:26
  14.1 140.0 %collective-permute-start.4 = (f32[2,4,32,3072]{3,2,1,0:T(8,128)}, f32[2,4,32,3072]{3,2,1,0:T(8,128)}, u32[]{:S(2)}, u32[]{:S(2)}) collective-permute-start(f32[2,4,32,3072]{3,2,1,0:T(8,128)} %param.4), channel_id=1, source_target_pairs={{0,384},{128,0},{256,128},{384,256},{1,385},{129,1},{257,129},{385... | collective-permute-start | bytes 9437192 | tf_op jit(solution)/shard_map/ppermute | solution.py:26
  16.9 144.1 %collective-permute-start = (f32[2,4,32,3072]{3,2,1,0:T(8,128)}, f32[2,4,32,3072]{3,2,1,0:T(8,128)S(1)}, u32[]{:S(2)}, u32[]{:S(2)}) collective-permute-start(f32[2,4,32,3072]{3,2,1,0:T(8,128)} %param.4), channel_id=1, source_target_pairs={{0,128},{128,256},{256,384},{384,0},{1,129},{129,257},{257,385},{3... | collective-permute-start | bytes 9437192 | tf_op jit(solution)/shard_map/ppermute | solution.py:26
  143.8 10.3 %copy-start = (f32[256,3072]{1,0:T(8,128)S(1)}, f32[256,3072]{1,0:T(8,128)}, u32[]{:S(2)}) copy-start(f32[256,3072]{1,0:T(8,128)} %all-gather.2.cloned.1.call-done) | copy-start | bytes 9437188
  149.5 21.5 %collective-permute-start.3 = (f32[256,256]{0,1:T(8,128)S(1)}, f32[256,256]{0,1:T(8,128)S(1)}, u32[]{:S(2)}, u32[]{:S(2)}) collective-permute-start(f32[256,256]{0,1:T(8,128)S(1)} %convolution_bitcast_fusion.2), channel_id=1, source_target_pairs={{0,256},{128,384},{256,0},{384,128},{1,257},{129,385},{257,1},{385... | collective-permute-start | bytes 786440 | tf_op jit(solution)/shard_map/ppermute | solution.py:26
  158.8 12.2 %collective-permute-start.5 = (f32[256,256]{0,1:T(8,128)S(1)}, f32[256,256]{0,1:T(8,128)S(1)}, u32[]{:S(2)}, u32[]{:S(2)}) collective-permute-start(f32[256,256]{0,1:T(8,128)S(1)} %convolution_bitcast_fusion.1), channel_id=1, source_target_pairs={{0,128},{128,256},{256,384},{384,0},{1,129},{129,257},{257,385},{3... | collective-permute-start | bytes 786440 | tf_op jit(solution)/shard_map/ppermute | solution.py:26
  161.0 7.3 %copy-start.1 = (f32[2,4,32,3072]{3,2,1,0:T(8,128)S(1)}, f32[2,4,32,3072]{3,2,1,0:T(8,128)}, u32[]{:S(2)}) copy-start(f32[2,4,32,3072]{3,2,1,0:T(8,128)} %param.4) | copy-start | bytes 9437188
  163.7 8.9 %collective-permute-start.1 = (f32[256,256]{0,1:T(8,128)S(1)}, f32[256,256]{0,1:T(8,128)S(1)}, u32[]{:S(2)}, u32[]{:S(2)}) collective-permute-start(f32[256,256]{0,1:T(8,128)S(1)} %convolution_bitcast_fusion.3), channel_id=1, source_target_pairs={{0,384},{128,0},{256,128},{384,256},{1,385},{129,1},{257,129},{385... | collective-permute-start | bytes 786440 | tf_op jit(solution)/shard_map/ppermute | solution.py:26
  171.0 2.1 copy-start.2
  200.1 20.6 %all-to-all-start.2 = ((f32[32,256,16]{1,2,0:T(8,128)}), f32[32,256,16]{1,2,0:T(8,128)S(1)}, u32[]{:S(2)}, u32[]{:S(2)}) async-start(f32[32,256,16]{1,2,0:T(8,128)} %get-tuple-element.6), calls=%async_computation.2 | async-start | bytes 1048576 | tf_op jit(solution)/shard_map/all_to_all | solution.py:67
  220.6 28.1 %all-to-all-start.1 = ((f32[16,1,256]{2,1,0:T(1,128)}), f32[16,1,256]{2,1,0:T(1,128)S(1)}, u32[]{:S(2)}, u32[]{:S(2)}) async-start(f32[16,1,256]{2,1,0:T(1,128)} %reshape.99), calls=%async_computation.1 | async-start | bytes 32768 | tf_op jit(solution)/shard_map/all_to_all | solution.py:69
  248.7 17.1 %all-to-all-start.3 = ((f32[16,1,256]{2,1,0:T(1,128)}), f32[16,1,256]{2,1,0:T(1,128)S(1)}, u32[]{:S(2)}, u32[]{:S(2)}) async-start(f32[16,1,256]{2,1,0:T(1,128)} %reshape.97), calls=%async_computation.3 | async-start | bytes 32768 | tf_op jit(solution)/shard_map/all_to_all | solution.py:69
Sparse Core Ops, SparseCore 0:
  9.5 134.3 all-gather.1

commit v4 on v3

--- a/solution.py
+++ b/solution.py
@@ -58,23 +58,17 @@
     keep_width = reordered.shape[1] // slab_count
     blades = phase_dev * lax.axis_size(PHASE)
     table = blade_table(blades, blades)
-    chains = 2
-    lane = keep_width // chains
-    spread = reordered.reshape(row_count, slab_count, chains, lane)
-    outs = []
-    for h in range(chains):
-        part = spread[:, :, h].transpose(1, 0, 2)
-        share = lax.all_to_all(part, SLAB, 0, 0, tiled=True).sum(axis=0)
-        forces = share.reshape(two, phase_dev, excite, lane)
-        gathered = lax.all_to_all(forces, PHASE, split_axis=2, concat_axis=1, tiled=True)
-        result = jnp.dot(
-            table,
-            gathered.reshape(2 * blades, -1),
-            precision=lax.Precision.HIGHEST,
-            preferred_element_type=jnp.float32,
-        )
-        outs.append(result.reshape(2, blades, -1, lane))
-    return jnp.concatenate(outs, axis=3)
+    spread = reordered.reshape(row_count, slab_count, keep_width).transpose(1, 0, 2)
+    share = lax.all_to_all(spread, SLAB, 0, 0, tiled=True).sum(axis=0)
+    forces = share.reshape(two, phase_dev, excite, keep_width)
+    gathered = lax.all_to_all(forces, PHASE, split_axis=2, concat_axis=1, tiled=True)
+    result = jnp.dot(
+        table,
+        gathered.reshape(2 * blades, -1),
+        precision=lax.Precision.HIGHEST,
+        preferred_element_type=jnp.float32,
+    )
+    return result.reshape(2, blades, -1, keep_width)
 
 
 def solution(mesh):

time: 276 us -> 250 us (0.906)
  blocking collectives: 25 us -> 0 us
    all_to_all x1 -> x0, blocking collectives: 25 us -> none  [shards(): share = lax.all_to_all(part, SLAB, 0, 0, tiled=True).sum(axis=0)]
    all_to_all x1, waiting for transfers between devices: 15.2 us -> 26.4 us  [shards(): share = lax.all_to_all(spread, SLAB, 0, 0, tiled=True).sum(axis=0)]
    all_to_all x2 -> x1, waiting for transfers between devices: 24.2 us -> 13.4 us  [shards(): lax.all_to_all(forces, PHASE, split_axis=2, concat_axis=1, tiled=True)]
    all_to_all x1, starting transfers between devices: 4.15 us -> 8.86 us  [shards(): share = lax.all_to_all(spread, SLAB, 0, 0, tiled=True).sum(axis=0)]
    all_to_all x2 -> x1, starting transfers between devices: 17.9 us -> 14.4 us  [shards(): lax.all_to_all(forces, PHASE, split_axis=2, concat_axis=1, tiled=True)]
  transfers between devices with their start and end apart: 10 -> 9, of which waited for: 6 -> 5; matrix products, arithmetic and copies ran while one was open for 7% -> 6% of each run, Pallas kernels for 0% -> 0%
where the time goes in v4:
time: 250 us; the launch traced here: 249 us
  waiting for transfers between devices  166 us (66%)
  starting transfers between devices  45.3 us (18%)
  matrix products  17.4 us (7%)
  between operations  13.7 us (5%)
  local copies, waits for them, and re-layouts  3.68 us (1%)
  other arithmetic  3.33 us (1%)
    all_gather x1, waiting for transfers between devices, shards(): column_modes = lax.all_gather(weighted, 'pz', axis=0, tiled=True)  65 us
    ppermute x6, waiting for transfers between devices, ring_shift(): lax.ppermute(value, axis, [(s, (s + shift) % size) for s in range(size)])  61 us
    all_to_all x1, waiting for transfers between devices, shards(): share = lax.all_to_all(spread, SLAB, 0, 0, tiled=True).sum(axis=0)  26.4 us
    ppermute x6, starting transfers between devices, ring_shift(): lax.ppermute(value, axis, [(s, (s + shift) % size) for s in range(size)])  22.1 us
    dot_general x4, matrix products, shards(): lax.dot_general(block.reshape(row_count, points), column_modes, (((1,), (...  15.8 us
    all_to_all x1, starting transfers between devices, shards(): lax.all_to_all(forces, PHASE, split_axis=2, concat_axis=1, tiled=True)  14.4 us
    all_to_all x1, waiting for transfers between devices, shards(): lax.all_to_all(forces, PHASE, split_axis=2, concat_axis=1, tiled=True)  13.4 us
    all_to_all x1, starting transfers between devices, shards(): share = lax.all_to_all(spread, SLAB, 0, 0, tiled=True).sum(axis=0)  8.86 us
  transfers between devices with their start and end apart: 9, of which 5 were waited for; matrix products, arithmetic and copies ran while one was open for 6% of the time, Pallas kernels for 0%

profile of v4, /device:TPU:1, one launch (start us, length us, event | category | flops | bytes accessed | tf_op | source)
XLA Modules:
  0.0 249.2 jit_solution(15554574859046208884)
XLA Ops:
  6.5 0.0 all-gather.2.cloned.1.call-start
  6.5 2.1 broadcast_multiply_fusion
  8.6 0.0 all-gather.2.cloned.1.call-update
  8.6 5.5 %collective-permute-start.2 = (f32[2,4,32,3072]{3,2,1,0:T(8,128)}, f32[2,4,32,3072]{3,2,1,0:T(8,128)}, u32[]{:S(2)}, u32[]{:S(2)}) collective-permute-start(f32[2,4,32,3072]{3,2,1,0:T(8,128)} %param.4), channel_id=1, source_target_pairs={{0,256},{128,384},{256,0},{384,128},{1,257},{129,385},{257,1},{385... | collective-permute-start | bytes 9437192 | tf_op jit(solution)/shard_map/ppermute | solution.py:26
  14.1 2.8 %collective-permute-start.4 = (f32[2,4,32,3072]{3,2,1,0:T(8,128)}, f32[2,4,32,3072]{3,2,1,0:T(8,128)}, u32[]{:S(2)}, u32[]{:S(2)}) collective-permute-start(f32[2,4,32,3072]{3,2,1,0:T(8,128)} %param.4), channel_id=1, source_target_pairs={{0,384},{128,0},{256,128},{384,256},{1,385},{129,1},{257,129},{385... | collective-permute-start | bytes 9437192 | tf_op jit(solution)/shard_map/ppermute | solution.py:26
  16.9 2.5 %collective-permute-start = (f32[2,4,32,3072]{3,2,1,0:T(8,128)}, f32[2,4,32,3072]{3,2,1,0:T(8,128)S(1)}, u32[]{:S(2)}, u32[]{:S(2)}) collective-permute-start(f32[2,4,32,3072]{3,2,1,0:T(8,128)} %param.4), channel_id=1, source_target_pairs={{0,128},{128,256},{256,384},{384,0},{1,129},{129,257},{257,385},{3... | collective-permute-start | bytes 9437192 | tf_op jit(solution)/shard_map/ppermute | solution.py:26
  19.5 59.4 %collective-permute-done.2 = f32[2,4,32,3072]{3,2,1,0:T(8,128)} collective-permute-done((f32[2,4,32,3072]{3,2,1,0:T(8,128)}, f32[2,4,32,3072]{3,2,1,0:T(8,128)}, u32[]{:S(2)}, u32[]{:S(2)}) %collective-permute-start.2) | collective-permute-done | bytes 3145760 | tf_op jit(solution)/shard_map/ppermute | solution.py:26
  78.8 65.0 %all-gather.2.cloned.1.call-done = f32[256,3072]{1,0:T(8,128)} async-done(((f32[64,3072]{1,0:T(8,128)}), f32[256,3072]{1,0:T(8,128)}) %all-gather.2.cloned.1.call-update) | async-done | bytes 3145744 | tf_op jit(solution)/shard_map/all_gather | solution.py:33
  143.8 0.0 copy-start
  143.8 5.7 %convolution_bitcast_fusion.2 = f32[256,256]{0,1:T(8,128)S(1)} fusion(f32[256,3072]{1,0:T(8,128)} %all-gather.2.cloned.1.call-done, f32[256,3072]{1,0:T(8,128)} %bitcast.10), kind=kOutput, calls=%fused_computation.2 | convolution fusion | flops 2415919104 | bytes 6553600 | tf_op jit(solution)/shard_map/dot_general | solution.py:39
  149.5 4.6 %collective-permute-start.3 = (f32[256,256]{0,1:T(8,128)S(1)}, f32[256,256]{0,1:T(8,128)S(1)}, u32[]{:S(2)}, u32[]{:S(2)}) collective-permute-start(f32[256,256]{0,1:T(8,128)S(1)} %convolution_bitcast_fusion.2), channel_id=1, source_target_pairs={{0,256},{128,384},{256,0},{384,128},{1,257},{129,385},{257,1},{385... | collective-permute-start | bytes 786440 | tf_op jit(solution)/shard_map/ppermute | solution.py:26
  154.1 0.0 collective-permute-done.4
  154.1 0.0 copy-done
  154.1 4.6 %convolution_bitcast_fusion.1 = f32[256,256]{0,1:T(8,128)S(1)} fusion(f32[256,3072]{1,0:T(8,128)S(1)} %copy-done, f32[256,3072]{1,0:T(8,128)} %bitcast.13), kind=kOutput, calls=%fused_computation.1 | convolution fusion | flops 2415919104 | bytes 6553600 | tf_op jit(solution)/shard_map/dot_general | solution.py:39
  158.8 2.2 collective-permute-start.5
  161.0 0.0 collective-permute-done
  161.0 0.0 copy-start.1
  161.0 2.7 %convolution_bitcast_fusion.3 = f32[256,256]{0,1:T(8,128)S(1)} fusion(f32[256,3072]{1,0:T(8,128)S(1)} %copy-done, f32[256,3072]{1,0:T(8,128)S(1)} %bitcast.55), kind=kOutput, calls=%fused_computation.3 | convolution fusion | flops 2415919104 | bytes 6553600 | tf_op jit(solution)/shard_map/dot_general | solution.py:39
  163.7 4.5 %collective-permute-start.1 = (f32[256,256]{0,1:T(8,128)S(1)}, f32[256,256]{0,1:T(8,128)S(1)}, u32[]{:S(2)}, u32[]{:S(2)}) collective-permute-start(f32[256,256]{0,1:T(8,128)S(1)} %convolution_bitcast_fusion.3), channel_id=1, source_target_pairs={{0,384},{128,0},{256,128},{384,256},{1,385},{129,1},{257,129},{385... | collective-permute-start | bytes 786440 | tf_op jit(solution)/shard_map/ppermute | solution.py:26
  168.2 0.0 copy-done.1
  168.2 2.7 %convolution_bitcast_fusion.4 = f32[256,1,256]{0,2,1:T(8,128)S(1)} fusion(f32[256,3072]{1,0:T(8,128)S(1)} %copy-done, f32[256,3072]{1,0:T(8,128)S(1)} %bitcast.54), kind=kOutput, calls=%fused_computation.4 | convolution fusion | flops 2415919104 | bytes 6553600 | tf_op jit(solution)/shard_map/dot_general | solution.py:39
  171.0 0.0 copy-start.2
  171.0 0.0 collective-permute-done.3
  171.0 0.0 collective-permute-done.5
  171.0 1.6 collective-permute-done.1
  172.6 0.1 pad_maximum_fusion
  172.7 0.4 copy.10
  173.1 0.0 copy-done.2
  173.1 0.6 convolution_bitcast_fusion
  173.8 1.4 copy.11
  175.1 8.9 %all-to-all-start = ((f32[32,256,32]{1,2,0:T(8,128)}), f32[32,256,32]{1,2,0:T(8,128)S(1)}, u32[]{:S(2)}, u32[]{:S(2)}) async-start(f32[32,256,32]{1,2,0:T(8,128)} %bitcast.19), calls=%async_computation | async-start | bytes 2097152 | tf_op jit(solution)/shard_map/all_to_all | solution.py:62
  184.0 0.1 fusion.6
  184.2 26.4 %all-to-all-done = f32[32,256,32]{1,2,0:T(8,128)S(1)} async-done(((f32[32,256,32]{1,2,0:T(8,128)}), f32[32,256,32]{1,2,0:T(8,128)S(1)}, u32[]{:S(2)}, u32[]{:S(2)}) %all-to-all-start) | async-done | bytes 1048608 | tf_op jit(solution)/shard_map/all_to_all | solution.py:62
  210.6 0.1 reduce_sum.9
  210.7 0.1 reshape.74
  210.8 0.1 copy.12
  210.9 0.8 reshape.79
  211.7 14.4 %all-to-all-start.1 = ((f32[16,1,512]{2,1,0:T(1,128)}), f32[16,1,512]{2,1,0:T(1,128)S(1)}, u32[]{:S(2)}, u32[]{:S(2)}) async-start(f32[16,1,512]{2,1,0:T(1,128)} %reshape.79), calls=%async_computation.1 | async-start | bytes 65536 | tf_op jit(solution)/shard_map/all_to_all | solution.py:64
  226.1 0.1 fusion.8
  226.3 0.1 maximum_multiply_fusion
  226.3 13.4 %all-to-all-done.1 = f32[16,1,512]{2,1,0:T(1,128)S(1)} async-done(((f32[16,1,512]{2,1,0:T(1,128)}), f32[16,1,512]{2,1,0:T(1,128)S(1)}, u32[]{:S(2)}, u32[]{:S(2)}) %all-to-all-start.1) | async-done | bytes 32800 | tf_op jit(solution)/shard_map/all_to_all | solution.py:64
  239.8 0.5 broadcast.109
  240.3 0.7 reduce
  241.0 0.1 reshape.80
  241.2 0.1 reshape.75
  241.3 0.1 copy.15
  241.4 1.0 fusion.17
  (3 shorter events, 0.1 us)
Async XLA Ops:
  6.5 137.3 %all-gather.2.cloned.1.call-start = ((), (), s32[]{:S(2)}) async-start(), calls=%async_computation.2 | async-start | bytes 3932160 | tf_op jit(solution)/shard_map/all_gather | solution.py:33
  8.6 70.2 %collective-permute-start.2 = (f32[2,4,32,3072]{3,2,1,0:T(8,128)}, f32[2,4,32,3072]{3,2,1,0:T(8,128)}, u32[]{:S(2)}, u32[]{:S(2)}) collective-permute-start(f32[2,4,32,3072]{3,2,1,0:T(8,128)} %param.4), channel_id=1, source_target_pairs={{0,256},{128,384},{256,0},{384,128},{1,257},{129,385},{257,1},{385... | collective-permute-start | bytes 9437192 | tf_op jit(solution)/shard_map/ppermute | solution.py:26
  14.1 140.0 %collective-permute-start.4 = (f32[2,4,32,3072]{3,2,1,0:T(8,128)}, f32[2,4,32,3072]{3,2,1,0:T(8,128)}, u32[]{:S(2)}, u32[]{:S(2)}) collective-permute-start(f32[2,4,32,3072]{3,2,1,0:T(8,128)} %param.4), channel_id=1, source_target_pairs={{0,384},{128,0},{256,128},{384,256},{1,385},{129,1},{257,129},{385... | collective-permute-start | bytes 9437192 | tf_op jit(solution)/shard_map/ppermute | solution.py:26
  16.9 144.1 %collective-permute-start = (f32[2,4,32,3072]{3,2,1,0:T(8,128)}, f32[2,4,32,3072]{3,2,1,0:T(8,128)S(1)}, u32[]{:S(2)}, u32[]{:S(2)}) collective-permute-start(f32[2,4,32,3072]{3,2,1,0:T(8,128)} %param.4), channel_id=1, source_target_pairs={{0,128},{128,256},{256,384},{384,0},{1,129},{129,257},{257,385},{3... | collective-permute-start | bytes 9437192 | tf_op jit(solution)/shard_map/ppermute | solution.py:26
  143.8 10.3 %copy-start = (f32[256,3072]{1,0:T(8,128)S(1)}, f32[256,3072]{1,0:T(8,128)}, u32[]{:S(2)}) copy-start(f32[256,3072]{1,0:T(8,128)} %all-gather.2.cloned.1.call-done) | copy-start | bytes 9437188
  149.5 21.5 %collective-permute-start.3 = (f32[256,256]{0,1:T(8,128)S(1)}, f32[256,256]{0,1:T(8,128)S(1)}, u32[]{:S(2)}, u32[]{:S(2)}) collective-permute-start(f32[256,256]{0,1:T(8,128)S(1)} %convolution_bitcast_fusion.2), channel_id=1, source_target_pairs={{0,256},{128,384},{256,0},{384,128},{1,257},{129,385},{257,1},{385... | collective-permute-start | bytes 786440 | tf_op jit(solution)/shard_map/ppermute | solution.py:26
  158.8 12.2 %collective-permute-start.5 = (f32[256,256]{0,1:T(8,128)S(1)}, f32[256,256]{0,1:T(8,128)S(1)}, u32[]{:S(2)}, u32[]{:S(2)}) collective-permute-start(f32[256,256]{0,1:T(8,128)S(1)} %convolution_bitcast_fusion.1), channel_id=1, source_target_pairs={{0,128},{128,256},{256,384},{384,0},{1,129},{129,257},{257,385},{3... | collective-permute-start | bytes 786440 | tf_op jit(solution)/shard_map/ppermute | solution.py:26
  161.0 7.3 %copy-start.1 = (f32[2,4,32,3072]{3,2,1,0:T(8,128)S(1)}, f32[2,4,32,3072]{3,2,1,0:T(8,128)}, u32[]{:S(2)}) copy-start(f32[2,4,32,3072]{3,2,1,0:T(8,128)} %param.4) | copy-start | bytes 9437188
  163.7 8.9 %collective-permute-start.1 = (f32[256,256]{0,1:T(8,128)S(1)}, f32[256,256]{0,1:T(8,128)S(1)}, u32[]{:S(2)}, u32[]{:S(2)}) collective-permute-start(f32[256,256]{0,1:T(8,128)S(1)} %convolution_bitcast_fusion.3), channel_id=1, source_target_pairs={{0,384},{128,0},{256,128},{384,256},{1,385},{129,1},{257,129},{385... | collective-permute-start | bytes 786440 | tf_op jit(solution)/shard_map/ppermute | solution.py:26
  171.0 2.1 copy-start.2
  175.1 35.5 %all-to-all-start = ((f32[32,256,32]{1,2,0:T(8,128)}), f32[32,256,32]{1,2,0:T(8,128)S(1)}, u32[]{:S(2)}, u32[]{:S(2)}) async-start(f32[32,256,32]{1,2,0:T(8,128)} %bitcast.19), calls=%async_computation | async-start | bytes 2097152 | tf_op jit(solution)/shard_map/all_to_all | solution.py:62
  211.7 28.1 %all-to-all-start.1 = ((f32[16,1,512]{2,1,0:T(1,128)}), f32[16,1,512]{2,1,0:T(1,128)S(1)}, u32[]{:S(2)}, u32[]{:S(2)}) async-start(f32[16,1,512]{2,1,0:T(1,128)} %reshape.79), calls=%async_computation.1 | async-start | bytes 65536 | tf_op jit(solution)/shard_map/all_to_all | solution.py:64
Sparse Core Ops, SparseCore 0:
  9.5 134.3 all-gather.1

commit v5 on v4

--- a/solution.py
+++ b/solution.py
@@ -40,7 +40,7 @@
             block.reshape(row_count, points),
             column_modes,
             (((1,), (1,)), ((), ())),
-            precision=lax.Precision.HIGHEST,
+            precision=lax.Precision.HIGH,
             preferred_element_type=jnp.float32,
         )
         pieces.append(partial if d == 0 else ring_shift(partial, "px", nx, -d))

time: 250 us -> 247 us (0.988)
  matrix products: 17.4 us -> 12.8 us
    dot_general x4, matrix products: 15.8 us -> 11.2 us  [shards(): lax.dot_general(block.reshape(row_count, points), column_modes, (((1,), (...]
  transfers between devices with their start and end apart: 9 -> 9, of which waited for: 5 -> 6; matrix products, arithmetic and copies ran while one was open for 6% -> 5% of each run, Pallas kernels for 0% -> 0%
where the time goes in v5:
time: 247 us
  waiting for transfers between devices  167 us (68%)
  starting transfers between devices  46.4 us (19%)
  between operations  13.6 us (6%)
  matrix products  12.8 us (5%)
  local copies, waits for them, and re-layouts  3.68 us (1%)
  other arithmetic  3.33 us (1%)
    all_gather x1, waiting for transfers between devices, shards(): column_modes = lax.all_gather(weighted, 'pz', axis=0, tiled=True)  65 us
    ppermute x6, waiting for transfers between devices, ring_shift(): lax.ppermute(value, axis, [(s, (s + shift) % size) for s in range(size)])  62.2 us
    all_to_all x1, waiting for transfers between devices, shards(): share = lax.all_to_all(spread, SLAB, 0, 0, tiled=True).sum(axis=0)  26.4 us
    ppermute x6, starting transfers between devices, ring_shift(): lax.ppermute(value, axis, [(s, (s + shift) % size) for s in range(size)])  21.9 us
    all_to_all x1, starting transfers between devices, shards(): lax.all_to_all(forces, PHASE, split_axis=2, concat_axis=1, tiled=True)  14.4 us
    all_to_all x1, waiting for transfers between devices, shards(): lax.all_to_all(forces, PHASE, split_axis=2, concat_axis=1, tiled=True)  13.4 us
    dot_general x4, matrix products, shards(): lax.dot_general(block.reshape(row_count, points), column_modes, (((1,), (...  11.2 us
    all_to_all x1, starting transfers between devices, shards(): share = lax.all_to_all(spread, SLAB, 0, 0, tiled=True).sum(axis=0)  10.1 us
  transfers between devices with their start and end apart: 9, of which 6 were waited for; matrix products, arithmetic and copies ran while one was open for 5% of the time, Pallas kernels for 0%

profile of v5, /device:TPU:1, one launch (start us, length us, event | category | flops | bytes accessed | tf_op | source)
XLA Modules:
  0.0 246.8 jit_solution(936945032618195162)
XLA Ops:
  6.5 0.0 all-gather.2.cloned.1.call-start
  6.5 2.1 broadcast_multiply_fusion
  8.6 0.0 all-gather.2.cloned.1.call-update
  8.6 5.5 %collective-permute-start.2 = (f32[2,4,32,3072]{3,2,1,0:T(8,128)}, f32[2,4,32,3072]{3,2,1,0:T(8,128)}, u32[]{:S(2)}, u32[]{:S(2)}) collective-permute-start(f32[2,4,32,3072]{3,2,1,0:T(8,128)} %param.4), channel_id=1, source_target_pairs={{0,256},{128,384},{256,0},{384,128},{1,257},{129,385},{257,1},{385... | collective-permute-start | bytes 9437192 | tf_op jit(solution)/shard_map/ppermute | solution.py:26
  14.1 2.8 %collective-permute-start.4 = (f32[2,4,32,3072]{3,2,1,0:T(8,128)}, f32[2,4,32,3072]{3,2,1,0:T(8,128)}, u32[]{:S(2)}, u32[]{:S(2)}) collective-permute-start(f32[2,4,32,3072]{3,2,1,0:T(8,128)} %param.4), channel_id=1, source_target_pairs={{0,384},{128,0},{256,128},{384,256},{1,385},{129,1},{257,129},{385... | collective-permute-start | bytes 9437192 | tf_op jit(solution)/shard_map/ppermute | solution.py:26
  16.9 2.5 %collective-permute-start = (f32[2,4,32,3072]{3,2,1,0:T(8,128)}, f32[2,4,32,3072]{3,2,1,0:T(8,128)S(1)}, u32[]{:S(2)}, u32[]{:S(2)}) collective-permute-start(f32[2,4,32,3072]{3,2,1,0:T(8,128)} %param.4), channel_id=1, source_target_pairs={{0,128},{128,256},{256,384},{384,0},{1,129},{129,257},{257,385},{3... | collective-permute-start | bytes 9437192 | tf_op jit(solution)/shard_map/ppermute | solution.py:26
  19.5 59.4 %collective-permute-done.2 = f32[2,4,32,3072]{3,2,1,0:T(8,128)} collective-permute-done((f32[2,4,32,3072]{3,2,1,0:T(8,128)}, f32[2,4,32,3072]{3,2,1,0:T(8,128)}, u32[]{:S(2)}, u32[]{:S(2)}) %collective-permute-start.2) | collective-permute-done | bytes 3145760 | tf_op jit(solution)/shard_map/ppermute | solution.py:26
  78.8 65.0 %all-gather.2.cloned.1.call-done = f32[256,3072]{1,0:T(8,128)} async-done(((f32[64,3072]{1,0:T(8,128)}), f32[256,3072]{1,0:T(8,128)}) %all-gather.2.cloned.1.call-update) | async-done | bytes 3145744 | tf_op jit(solution)/shard_map/all_gather | solution.py:33
  143.8 0.0 copy-start
  143.8 4.5 %convolution_bitcast_fusion.2 = f32[256,256]{0,1:T(8,128)S(1)} fusion(f32[256,3072]{1,0:T(8,128)} %all-gather.2.cloned.1.call-done, f32[256,3072]{1,0:T(8,128)} %bitcast.10), kind=kOutput, calls=%fused_computation.2 | convolution fusion | flops 1207959552 | bytes 6553600 | tf_op jit(solution)/shard_map/dot_general | solution.py:39
  148.3 4.6 %collective-permute-start.3 = (f32[256,256]{0,1:T(8,128)S(1)}, f32[256,256]{0,1:T(8,128)S(1)}, u32[]{:S(2)}, u32[]{:S(2)}) collective-permute-start(f32[256,256]{0,1:T(8,128)S(1)} %convolution_bitcast_fusion.2), channel_id=1, source_target_pairs={{0,256},{128,384},{256,0},{384,128},{1,257},{129,385},{257,1},{385... | collective-permute-start | bytes 786440 | tf_op jit(solution)/shard_map/ppermute | solution.py:26
  152.9 0.0 collective-permute-done.4
  152.9 0.0 copy-done
  152.9 3.4 %convolution_bitcast_fusion.1 = f32[256,256]{0,1:T(8,128)S(1)} fusion(f32[256,3072]{1,0:T(8,128)S(1)} %copy-done, f32[256,3072]{1,0:T(8,128)} %bitcast.13), kind=kOutput, calls=%fused_computation.1 | convolution fusion | flops 1207959552 | bytes 6553600 | tf_op jit(solution)/shard_map/dot_general | solution.py:39
  156.4 2.2 collective-permute-start.5
  158.6 0.0 collective-permute-done
  158.6 0.0 copy-start.1
  158.6 1.6 convolution_bitcast_fusion.3
  160.1 4.3 %collective-permute-start.1 = (f32[256,256]{0,1:T(8,128)S(1)}, f32[256,256]{0,1:T(8,128)S(1)}, u32[]{:S(2)}, u32[]{:S(2)}) collective-permute-start(f32[256,256]{0,1:T(8,128)S(1)} %convolution_bitcast_fusion.3), channel_id=1, source_target_pairs={{0,384},{128,0},{256,128},{384,256},{1,385},{129,1},{257,129},{385... | collective-permute-start | bytes 786440 | tf_op jit(solution)/shard_map/ppermute | solution.py:26
  164.5 0.0 copy-done.1
  164.5 1.7 convolution_bitcast_fusion.4
  166.2 0.0 copy-start.2
  166.2 0.0 collective-permute-done.3
  166.2 0.4 collective-permute-done.5
  166.6 2.4 collective-permute-done.1
  169.0 0.1 pad_maximum_fusion
  169.1 0.4 copy.10
  169.5 0.0 copy-done.2
  169.5 0.6 convolution_bitcast_fusion
  170.2 1.4 copy.11
  171.5 10.1 %all-to-all-start = ((f32[32,256,32]{1,2,0:T(8,128)}), f32[32,256,32]{1,2,0:T(8,128)S(1)}, u32[]{:S(2)}, u32[]{:S(2)}) async-start(f32[32,256,32]{1,2,0:T(8,128)} %bitcast.19), calls=%async_computation | async-start | bytes 2097152 | tf_op jit(solution)/shard_map/all_to_all | solution.py:62
  181.6 0.1 fusion.6
  181.8 26.4 %all-to-all-done = f32[32,256,32]{1,2,0:T(8,128)S(1)} async-done(((f32[32,256,32]{1,2,0:T(8,128)}), f32[32,256,32]{1,2,0:T(8,128)S(1)}, u32[]{:S(2)}, u32[]{:S(2)}) %all-to-all-start) | async-done | bytes 1048608 | tf_op jit(solution)/shard_map/all_to_all | solution.py:62
  208.2 0.1 reduce_sum.9
  208.3 0.1 reshape.74
  208.4 0.1 copy.12
  208.5 0.8 reshape.79
  209.3 14.4 %all-to-all-start.1 = ((f32[16,1,512]{2,1,0:T(1,128)}), f32[16,1,512]{2,1,0:T(1,128)S(1)}, u32[]{:S(2)}, u32[]{:S(2)}) async-start(f32[16,1,512]{2,1,0:T(1,128)} %reshape.79), calls=%async_computation.1 | async-start | bytes 65536 | tf_op jit(solution)/shard_map/all_to_all | solution.py:64
  223.7 0.1 fusion.8
  223.9 0.1 maximum_multiply_fusion
  224.0 13.4 %all-to-all-done.1 = f32[16,1,512]{2,1,0:T(1,128)S(1)} async-done(((f32[16,1,512]{2,1,0:T(1,128)}), f32[16,1,512]{2,1,0:T(1,128)S(1)}, u32[]{:S(2)}, u32[]{:S(2)}) %all-to-all-start.1) | async-done | bytes 32800 | tf_op jit(solution)/shard_map/all_to_all | solution.py:64
  237.4 0.5 broadcast.109
  237.9 0.7 reduce
  238.6 0.1 reshape.80
  238.8 0.1 reshape.75
  239.0 0.1 copy.15
  239.0 1.0 fusion.17
  (3 shorter events, 0.1 us)
Async XLA Ops:
  6.5 137.3 %all-gather.2.cloned.1.call-start = ((), (), s32[]{:S(2)}) async-start(), calls=%async_computation.2 | async-start | bytes 3932160 | tf_op jit(solution)/shard_map/all_gather | solution.py:33
  8.6 70.2 %collective-permute-start.2 = (f32[2,4,32,3072]{3,2,1,0:T(8,128)}, f32[2,4,32,3072]{3,2,1,0:T(8,128)}, u32[]{:S(2)}, u32[]{:S(2)}) collective-permute-start(f32[2,4,32,3072]{3,2,1,0:T(8,128)} %param.4), channel_id=1, source_target_pairs={{0,256},{128,384},{256,0},{384,128},{1,257},{129,385},{257,1},{385... | collective-permute-start | bytes 9437192 | tf_op jit(solution)/shard_map/ppermute | solution.py:26
  14.1 138.8 %collective-permute-start.4 = (f32[2,4,32,3072]{3,2,1,0:T(8,128)}, f32[2,4,32,3072]{3,2,1,0:T(8,128)}, u32[]{:S(2)}, u32[]{:S(2)}) collective-permute-start(f32[2,4,32,3072]{3,2,1,0:T(8,128)} %param.4), channel_id=1, source_target_pairs={{0,384},{128,0},{256,128},{384,256},{1,385},{129,1},{257,129},{385... | collective-permute-start | bytes 9437192 | tf_op jit(solution)/shard_map/ppermute | solution.py:26
  16.9 141.6 %collective-permute-start = (f32[2,4,32,3072]{3,2,1,0:T(8,128)}, f32[2,4,32,3072]{3,2,1,0:T(8,128)S(1)}, u32[]{:S(2)}, u32[]{:S(2)}) collective-permute-start(f32[2,4,32,3072]{3,2,1,0:T(8,128)} %param.4), channel_id=1, source_target_pairs={{0,128},{128,256},{256,384},{384,0},{1,129},{129,257},{257,385},{3... | collective-permute-start | bytes 9437192 | tf_op jit(solution)/shard_map/ppermute | solution.py:26
  143.8 9.1 %copy-start = (f32[256,3072]{1,0:T(8,128)S(1)}, f32[256,3072]{1,0:T(8,128)}, u32[]{:S(2)}) copy-start(f32[256,3072]{1,0:T(8,128)} %all-gather.2.cloned.1.call-done) | copy-start | bytes 9437188
  148.3 17.9 %collective-permute-start.3 = (f32[256,256]{0,1:T(8,128)S(1)}, f32[256,256]{0,1:T(8,128)S(1)}, u32[]{:S(2)}, u32[]{:S(2)}) collective-permute-start(f32[256,256]{0,1:T(8,128)S(1)} %convolution_bitcast_fusion.2), channel_id=1, source_target_pairs={{0,256},{128,384},{256,0},{384,128},{1,257},{129,385},{257,1},{385... | collective-permute-start | bytes 786440 | tf_op jit(solution)/shard_map/ppermute | solution.py:26
  156.4 10.2 %collective-permute-start.5 = (f32[256,256]{0,1:T(8,128)S(1)}, f32[256,256]{0,1:T(8,128)S(1)}, u32[]{:S(2)}, u32[]{:S(2)}) collective-permute-start(f32[256,256]{0,1:T(8,128)S(1)} %convolution_bitcast_fusion.1), channel_id=1, source_target_pairs={{0,128},{128,256},{256,384},{384,0},{1,129},{129,257},{257,385},{3... | collective-permute-start | bytes 786440 | tf_op jit(solution)/shard_map/ppermute | solution.py:26
  158.6 5.9 %copy-start.1 = (f32[2,4,32,3072]{3,2,1,0:T(8,128)S(1)}, f32[2,4,32,3072]{3,2,1,0:T(8,128)}, u32[]{:S(2)}) copy-start(f32[2,4,32,3072]{3,2,1,0:T(8,128)} %param.4) | copy-start | bytes 9437188
  160.1 8.9 %collective-permute-start.1 = (f32[256,256]{0,1:T(8,128)S(1)}, f32[256,256]{0,1:T(8,128)S(1)}, u32[]{:S(2)}, u32[]{:S(2)}) collective-permute-start(f32[256,256]{0,1:T(8,128)S(1)} %convolution_bitcast_fusion.3), channel_id=1, source_target_pairs={{0,384},{128,0},{256,128},{384,256},{1,385},{129,1},{257,129},{385... | collective-permute-start | bytes 786440 | tf_op jit(solution)/shard_map/ppermute | solution.py:26
  166.2 3.3 %copy-start.2 = (s32[8]{0:T(128)S(1)}, s32[8]{0:T(128)}, u32[]{:S(2)}) copy-start(s32[8]{0:T(128)} %param.7) | copy-start | bytes 100
  171.5 36.7 %all-to-all-start = ((f32[32,256,32]{1,2,0:T(8,128)}), f32[32,256,32]{1,2,0:T(8,128)S(1)}, u32[]{:S(2)}, u32[]{:S(2)}) async-start(f32[32,256,32]{1,2,0:T(8,128)} %bitcast.19), calls=%async_computation | async-start | bytes 2097152 | tf_op jit(solution)/shard_map/all_to_all | solution.py:62
  209.3 28.1 %all-to-all-start.1 = ((f32[16,1,512]{2,1,0:T(1,128)}), f32[16,1,512]{2,1,0:T(1,128)S(1)}, u32[]{:S(2)}, u32[]{:S(2)}) async-start(f32[16,1,512]{2,1,0:T(1,128)} %reshape.79), calls=%async_computation.1 | async-start | bytes 65536 | tf_op jit(solution)/shard_map/all_to_all | solution.py:64
Sparse Core Ops, SparseCore 0:
  9.5 134.3 all-gather.1

commit v6 on v4

--- a/solution.py
+++ b/solution.py
@@ -58,8 +58,13 @@
     keep_width = reordered.shape[1] // slab_count
     blades = phase_dev * lax.axis_size(PHASE)
     table = blade_table(blades, blades)
-    spread = reordered.reshape(row_count, slab_count, keep_width).transpose(1, 0, 2)
-    share = lax.all_to_all(spread, SLAB, 0, 0, tiled=True).sum(axis=0)
+    cores = lax.axis_size("sc")
+    ci = lax.axis_index("sc")
+    spread = reordered.reshape(row_count, slab_count // cores, cores, keep_width)
+    mine = jnp.take(spread, ci, axis=2)
+    other = jnp.take(spread, 1 - ci, axis=2)
+    paired = mine + lax.ppermute(other, "sc", [(0, 1), (1, 0)])
+    share = lax.all_to_all(paired.transpose(1, 0, 2), ("sz", "sy"), 0, 0, tiled=True).sum(axis=0)
     forces = share.reshape(two, phase_dev, excite, keep_width)
     gathered = lax.all_to_all(forces, PHASE, split_axis=2, concat_axis=1, tiled=True)
     result = jnp.dot(

time: 250 us -> 242 us (0.968)
  waiting for transfers between devices: 166 us -> 155 us
    all_to_all x1, waiting for transfers between devices: 26.4 us -> 14 us  [shards(): lax.all_to_all(paired.transpose(1, 0, 2), ('sz', 'sy'), 0, 0, tiled=True)]
    ppermute x0 -> x1, starting transfers between devices: none -> 3.84 us  [shards(): paired = mine + lax.ppermute(other, 'sc', [(0, 1), (1, 0)])]
  transfers between devices with their start and end apart: 9 -> 10, of which waited for: 5 -> 6; matrix products, arithmetic and copies ran while one was open for 6% -> 7% of each run, Pallas kernels for 0% -> 0%
where the time goes in v6:
time: 242 us; the launch traced here: 240 us
  waiting for transfers between devices  155 us (64%)
  starting transfers between devices  46.9 us (19%)
  matrix products  17.4 us (7%)
  between operations  13.7 us (6%)
  other arithmetic  4.23 us (2%)
  local copies, waits for them, and re-layouts  2.7 us (1%)
    all_gather x1, waiting for transfers between devices, shards(): column_modes = lax.all_gather(weighted, 'pz', axis=0, tiled=True)  65 us
    ppermute x6, waiting for transfers between devices, ring_shift(): lax.ppermute(value, axis, [(s, (s + shift) % size) for s in range(size)])  61 us
    ppermute x6, starting transfers between devices, ring_shift(): lax.ppermute(value, axis, [(s, (s + shift) % size) for s in range(size)])  22.1 us
    dot_general x4, matrix products, shards(): lax.dot_general(block.reshape(row_count, points), column_modes, (((1,), (...  15.8 us
    all_to_all x1, starting transfers between devices, shards(): lax.all_to_all(forces, PHASE, split_axis=2, concat_axis=1, tiled=True)  14.4 us
    all_to_all x1, waiting for transfers between devices, shards(): lax.all_to_all(paired.transpose(1, 0, 2), ('sz', 'sy'), 0, 0, tiled=True)  14 us
    all_to_all x1, waiting for transfers between devices, shards(): lax.all_to_all(forces, PHASE, split_axis=2, concat_axis=1, tiled=True)  13.4 us
    all_to_all x1, starting transfers between devices, shards(): lax.all_to_all(paired.transpose(1, 0, 2), ('sz', 'sy'), 0, 0, tiled=True)  6.59 us
  transfers between devices with their start and end apart: 10, of which 6 were waited for; matrix products, arithmetic and copies ran while one was open for 7% of the time, Pallas kernels for 0%

profile of v6, /device:TPU:1, one launch (start us, length us, event | category | flops | bytes accessed | tf_op | source)
XLA Modules:
  0.0 239.8 jit_solution(12172545990127300972)
XLA Ops:
  6.5 0.0 all-gather.2.cloned.1.call-start
  6.5 2.1 broadcast_multiply_fusion
  8.6 0.0 all-gather.2.cloned.1.call-update
  8.6 5.5 %collective-permute-start.2 = (f32[2,4,32,3072]{3,2,1,0:T(8,128)}, f32[2,4,32,3072]{3,2,1,0:T(8,128)}, u32[]{:S(2)}, u32[]{:S(2)}) collective-permute-start(f32[2,4,32,3072]{3,2,1,0:T(8,128)} %param.6), channel_id=1, source_target_pairs={{0,256},{128,384},{256,0},{384,128},{1,257},{129,385},{257,1},{385... | collective-permute-start | bytes 9437192 | tf_op jit(solution)/shard_map/ppermute | solution.py:26
  14.1 2.8 %collective-permute-start.4 = (f32[2,4,32,3072]{3,2,1,0:T(8,128)}, f32[2,4,32,3072]{3,2,1,0:T(8,128)}, u32[]{:S(2)}, u32[]{:S(2)}) collective-permute-start(f32[2,4,32,3072]{3,2,1,0:T(8,128)} %param.6), channel_id=1, source_target_pairs={{0,384},{128,0},{256,128},{384,256},{1,385},{129,1},{257,129},{385... | collective-permute-start | bytes 9437192 | tf_op jit(solution)/shard_map/ppermute | solution.py:26
  16.9 2.5 %collective-permute-start = (f32[2,4,32,3072]{3,2,1,0:T(8,128)}, f32[2,4,32,3072]{3,2,1,0:T(8,128)S(1)}, u32[]{:S(2)}, u32[]{:S(2)}) collective-permute-start(f32[2,4,32,3072]{3,2,1,0:T(8,128)} %param.6), channel_id=1, source_target_pairs={{0,128},{128,256},{256,384},{384,0},{1,129},{129,257},{257,385},{3... | collective-permute-start | bytes 9437192 | tf_op jit(solution)/shard_map/ppermute | solution.py:26
  19.5 59.4 %collective-permute-done.2 = f32[2,4,32,3072]{3,2,1,0:T(8,128)} collective-permute-done((f32[2,4,32,3072]{3,2,1,0:T(8,128)}, f32[2,4,32,3072]{3,2,1,0:T(8,128)}, u32[]{:S(2)}, u32[]{:S(2)}) %collective-permute-start.2) | collective-permute-done | bytes 3145760 | tf_op jit(solution)/shard_map/ppermute | solution.py:26
  78.8 65.0 %all-gather.2.cloned.1.call-done = f32[256,3072]{1,0:T(8,128)} async-done(((f32[64,3072]{1,0:T(8,128)}), f32[256,3072]{1,0:T(8,128)}) %all-gather.2.cloned.1.call-update) | async-done | bytes 3145744 | tf_op jit(solution)/shard_map/all_gather | solution.py:33
  143.8 5.7 %convolution_bitcast_fusion.2 = f32[256,256]{0,1:T(8,128)S(1)} fusion(f32[256,3072]{1,0:T(8,128)} %all-gather.2.cloned.1.call-done, f32[256,3072]{1,0:T(8,128)} %bitcast.10), kind=kOutput, calls=%fused_computation.2 | convolution fusion | flops 2415919104 | bytes 6553600 | tf_op jit(solution)/shard_map/dot_general | solution.py:39
  149.5 4.6 %collective-permute-start.3 = (f32[256,256]{0,1:T(8,128)S(1)}, f32[256,256]{0,1:T(8,128)S(1)}, u32[]{:S(2)}, u32[]{:S(2)}) collective-permute-start(f32[256,256]{0,1:T(8,128)S(1)} %convolution_bitcast_fusion.2), channel_id=1, source_target_pairs={{0,256},{128,384},{256,0},{384,128},{1,257},{129,385},{257,1},{385... | collective-permute-start | bytes 786440 | tf_op jit(solution)/shard_map/ppermute | solution.py:26
  154.1 0.0 collective-permute-done.4
  154.1 0.0 copy-done
  154.1 4.6 %convolution_bitcast_fusion.1 = f32[256,256]{0,1:T(8,128)S(1)} fusion(f32[256,3072]{1,0:T(8,128)S(1)} %copy-done, f32[256,3072]{1,0:T(8,128)} %bitcast.13), kind=kOutput, calls=%fused_computation.1 | convolution fusion | flops 2415919104 | bytes 6553600 | tf_op jit(solution)/shard_map/dot_general | solution.py:39
  158.8 2.2 collective-permute-start.5
  161.0 0.0 collective-permute-done
  161.0 0.0 copy-start.1
  161.0 2.7 %convolution_bitcast_fusion.3 = f32[256,256]{0,1:T(8,128)S(1)} fusion(f32[256,3072]{1,0:T(8,128)S(1)} %copy-done, f32[256,3072]{1,0:T(8,128)S(1)} %bitcast.73), kind=kOutput, calls=%fused_computation.3 | convolution fusion | flops 2415919104 | bytes 6553600 | tf_op jit(solution)/shard_map/dot_general | solution.py:39
  163.7 4.5 %collective-permute-start.1 = (f32[256,256]{0,1:T(8,128)S(1)}, f32[256,256]{0,1:T(8,128)S(1)}, u32[]{:S(2)}, u32[]{:S(2)}) collective-permute-start(f32[256,256]{0,1:T(8,128)S(1)} %convolution_bitcast_fusion.3), channel_id=1, source_target_pairs={{0,384},{128,0},{256,128},{384,256},{1,385},{129,1},{257,129},{385... | collective-permute-start | bytes 786440 | tf_op jit(solution)/shard_map/ppermute | solution.py:26
  168.2 0.0 copy-done.1
  168.2 2.7 %convolution_bitcast_fusion.4 = f32[256,1,256]{0,2,1:T(8,128)S(1)} fusion(f32[256,3072]{1,0:T(8,128)S(1)} %copy-done, f32[256,3072]{1,0:T(8,128)S(1)} %bitcast.72), kind=kOutput, calls=%fused_computation.4 | convolution fusion | flops 2415919104 | bytes 6553600 | tf_op jit(solution)/shard_map/dot_general | solution.py:39
  171.0 0.0 copy-start.2
  171.0 0.0 collective-permute-done.3
  171.0 0.0 collective-permute-done.5
  171.0 1.6 collective-permute-done.1
  172.6 0.1 pad_maximum_fusion
  172.7 0.4 copy.12
  173.1 0.6 convolution_bitcast_fusion
  173.8 0.4 copy.13
  174.2 0.1 select_bitcast_fusion
  174.2 3.8 %collective-permute-start.6 = (f32[256,16,32]{0,2,1:T(8,128)S(1)}, f32[256,16,32]{0,2,1:T(8,128)S(1)}, u32[]{:S(2)}, u32[]{:S(2)}) collective-permute-start(f32[256,16,32]{0,2,1:T(8,128)S(1)} %select_bitcast_fusion), channel_id=1, source_target_pairs={{0,1},{1,0},{2,3},{3,2},{4,5},{5,4},{6,7},{7,6},{8,9},{9,8},{10,11... | collective-permute-start | bytes 1572872 | tf_op jit(solution)/shard_map/ppermute | solution.py:66
  178.1 1.5 collective-permute-done.6
  179.6 0.9 fusion.2
  180.5 6.6 %all-to-all-start = ((f32[16,256,32]{1,2,0:T(8,128)}), f32[16,256,32]{1,2,0:T(8,128)S(1)}, u32[]{:S(2)}, u32[]{:S(2)}) async-start(f32[16,256,32]{1,2,0:T(8,128)} %fusion.2), calls=%async_computation | async-start | bytes 1048576 | tf_op jit(solution)/shard_map/all_to_all | solution.py:67
  187.1 0.1 fusion.9
  187.2 14.0 %all-to-all-done = f32[16,256,32]{1,2,0:T(8,128)S(1)} async-done(((f32[16,256,32]{1,2,0:T(8,128)}), f32[16,256,32]{1,2,0:T(8,128)S(1)}, u32[]{:S(2)}, u32[]{:S(2)}) %all-to-all-start) | async-done | bytes 524320 | tf_op jit(solution)/shard_map/all_to_all | solution.py:67
  201.2 0.1 reshape.75
  201.4 0.1 copy.15
  201.5 0.8 reshape.139
  202.2 14.4 %all-to-all-start.1 = ((f32[16,1,512]{2,1,0:T(1,128)}), f32[16,1,512]{2,1,0:T(1,128)S(1)}, u32[]{:S(2)}, u32[]{:S(2)}) async-start(f32[16,1,512]{2,1,0:T(1,128)} %reshape.139), calls=%async_computation.1 | async-start | bytes 65536 | tf_op jit(solution)/shard_map/all_to_all | solution.py:69
  216.7 0.1 fusion.11
  216.8 0.1 maximum_multiply_fusion
  216.9 13.4 %all-to-all-done.1 = f32[16,1,512]{2,1,0:T(1,128)S(1)} async-done(((f32[16,1,512]{2,1,0:T(1,128)}), f32[16,1,512]{2,1,0:T(1,128)S(1)}, u32[]{:S(2)}, u32[]{:S(2)}) %all-to-all-start.1) | async-done | bytes 32800 | tf_op jit(solution)/shard_map/all_to_all | solution.py:69
  230.4 0.5 broadcast.154
  230.9 0.7 reduce
  231.6 0.1 reshape.140
  231.8 0.1 reshape.76
  231.9 0.1 copy.18
  232.0 1.0 fusion.20
  (6 shorter events, 0.1 us)
Async XLA Ops:
  6.5 137.3 %all-gather.2.cloned.1.call-start = ((), (), s32[]{:S(2)}) async-start(), calls=%async_computation.2 | async-start | bytes 3932160 | tf_op jit(solution)/shard_map/all_gather | solution.py:33
  8.6 70.2 %collective-permute-start.2 = (f32[2,4,32,3072]{3,2,1,0:T(8,128)}, f32[2,4,32,3072]{3,2,1,0:T(8,128)}, u32[]{:S(2)}, u32[]{:S(2)}) collective-permute-start(f32[2,4,32,3072]{3,2,1,0:T(8,128)} %param.6), channel_id=1, source_target_pairs={{0,256},{128,384},{256,0},{384,128},{1,257},{129,385},{257,1},{385... | collective-permute-start | bytes 9437192 | tf_op jit(solution)/shard_map/ppermute | solution.py:26
  14.1 140.0 %collective-permute-start.4 = (f32[2,4,32,3072]{3,2,1,0:T(8,128)}, f32[2,4,32,3072]{3,2,1,0:T(8,128)}, u32[]{:S(2)}, u32[]{:S(2)}) collective-permute-start(f32[2,4,32,3072]{3,2,1,0:T(8,128)} %param.6), channel_id=1, source_target_pairs={{0,384},{128,0},{256,128},{384,256},{1,385},{129,1},{257,129},{385... | collective-permute-start | bytes 9437192 | tf_op jit(solution)/shard_map/ppermute | solution.py:26
  16.9 144.1 %collective-permute-start = (f32[2,4,32,3072]{3,2,1,0:T(8,128)}, f32[2,4,32,3072]{3,2,1,0:T(8,128)S(1)}, u32[]{:S(2)}, u32[]{:S(2)}) collective-permute-start(f32[2,4,32,3072]{3,2,1,0:T(8,128)} %param.6), channel_id=1, source_target_pairs={{0,128},{128,256},{256,384},{384,0},{1,129},{129,257},{257,385},{3... | collective-permute-start | bytes 9437192 | tf_op jit(solution)/shard_map/ppermute | solution.py:26
  143.8 10.3 %copy-start = (f32[256,3072]{1,0:T(8,128)S(1)}, f32[256,3072]{1,0:T(8,128)}, u32[]{:S(2)}) copy-start(f32[256,3072]{1,0:T(8,128)} %all-gather.2.cloned.1.call-done) | copy-start | bytes 9437188
  149.5 21.5 %collective-permute-start.3 = (f32[256,256]{0,1:T(8,128)S(1)}, f32[256,256]{0,1:T(8,128)S(1)}, u32[]{:S(2)}, u32[]{:S(2)}) collective-permute-start(f32[256,256]{0,1:T(8,128)S(1)} %convolution_bitcast_fusion.2), channel_id=1, source_target_pairs={{0,256},{128,384},{256,0},{384,128},{1,257},{129,385},{257,1},{385... | collective-permute-start | bytes 786440 | tf_op jit(solution)/shard_map/ppermute | solution.py:26
  158.8 12.2 %collective-permute-start.5 = (f32[256,256]{0,1:T(8,128)S(1)}, f32[256,256]{0,1:T(8,128)S(1)}, u32[]{:S(2)}, u32[]{:S(2)}) collective-permute-start(f32[256,256]{0,1:T(8,128)S(1)} %convolution_bitcast_fusion.1), channel_id=1, source_target_pairs={{0,128},{128,256},{256,384},{384,0},{1,129},{129,257},{257,385},{3... | collective-permute-start | bytes 786440 | tf_op jit(solution)/shard_map/ppermute | solution.py:26
  161.0 7.3 %copy-start.1 = (f32[2,4,32,3072]{3,2,1,0:T(8,128)S(1)}, f32[2,4,32,3072]{3,2,1,0:T(8,128)}, u32[]{:S(2)}) copy-start(f32[2,4,32,3072]{3,2,1,0:T(8,128)} %param.6) | copy-start | bytes 9437188
  163.7 8.9 %collective-permute-start.1 = (f32[256,256]{0,1:T(8,128)S(1)}, f32[256,256]{0,1:T(8,128)S(1)}, u32[]{:S(2)}, u32[]{:S(2)}) collective-permute-start(f32[256,256]{0,1:T(8,128)S(1)} %convolution_bitcast_fusion.3), channel_id=1, source_target_pairs={{0,384},{128,0},{256,128},{384,256},{1,385},{129,1},{257,129},{385... | collective-permute-start | bytes 786440 | tf_op jit(solution)/shard_map/ppermute | solution.py:26
  171.0 2.1 copy-start.2
  174.2 5.4 %collective-permute-start.6 = (f32[256,16,32]{0,2,1:T(8,128)S(1)}, f32[256,16,32]{0,2,1:T(8,128)S(1)}, u32[]{:S(2)}, u32[]{:S(2)}) collective-permute-start(f32[256,16,32]{0,2,1:T(8,128)S(1)} %select_bitcast_fusion), channel_id=1, source_target_pairs={{0,1},{1,0},{2,3},{3,2},{4,5},{5,4},{6,7},{7,6},{8,9},{9,8},{10,11... | collective-permute-start | bytes 1572872 | tf_op jit(solution)/shard_map/ppermute | solution.py:66
  180.5 20.7 %all-to-all-start = ((f32[16,256,32]{1,2,0:T(8,128)}), f32[16,256,32]{1,2,0:T(8,128)S(1)}, u32[]{:S(2)}, u32[]{:S(2)}) async-start(f32[16,256,32]{1,2,0:T(8,128)} %fusion.2), calls=%async_computation | async-start | bytes 1048576 | tf_op jit(solution)/shard_map/all_to_all | solution.py:67
  202.2 28.1 %all-to-all-start.1 = ((f32[16,1,512]{2,1,0:T(1,128)}), f32[16,1,512]{2,1,0:T(1,128)S(1)}, u32[]{:S(2)}, u32[]{:S(2)}) async-start(f32[16,1,512]{2,1,0:T(1,128)} %reshape.139), calls=%async_computation.1 | async-start | bytes 65536 | tf_op jit(solution)/shard_map/all_to_all | solution.py:69
Sparse Core Ops, SparseCore 0:
  9.5 134.3 all-gather.1

commit v7 on v6

--- a/solution.py
+++ b/solution.py
@@ -30,19 +30,31 @@
     nx = lax.axis_size("px")
     xi = lax.axis_index("px")
     weighted = mode_shapes * point_weight[None, :]
-    column_modes = lax.all_gather(weighted, "pz", axis=0, tiled=True)
+    halves = 2
+    half_rows = weighted.shape[0] // halves
+    column_halves = [
+        lax.all_gather(weighted[h * half_rows:(h + 1) * half_rows], "pz", axis=0, tiled=True)
+        for h in range(halves)
+    ]
+    nz = lax.axis_size("pz")
     ring = [pressure] + [ring_shift(pressure, "px", nx, d) for d in range(1, nx)]
     two, phase_dev, excite, points = pressure.shape
     row_count = two * phase_dev * excite
     pieces = []
     for d, block in enumerate(ring):
-        partial = lax.dot_general(
-            block.reshape(row_count, points),
-            column_modes,
-            (((1,), (1,)), ((), ())),
-            precision=lax.Precision.HIGHEST,
-            preferred_element_type=jnp.float32,
-        )
+        partial = jnp.stack(
+            [
+                lax.dot_general(
+                    block.reshape(row_count, points),
+                    column_half,
+                    (((1,), (1,)), ((), ())),
+                    precision=lax.Precision.HIGHEST,
+                    preferred_element_type=jnp.float32,
+                ).reshape(row_count, nz, half_rows)
+                for column_half in column_halves
+            ],
+            axis=2,
+        ).reshape(row_count, -1)
         pieces.append(partial if d == 0 else ring_shift(partial, "px", nx, -d))
     own = jnp.stack(pieces, axis=1)
     panel_count = panel_order.shape[0]

time: 242 us -> 271 us (1.12)
  matrix products: 17.4 us -> 43.9 us
  waiting for transfers between devices: 155 us -> 166 us
  starting transfers between devices: 46.9 us -> 38.4 us
    all_gather x1 -> x2, waiting for transfers between devices: 65 us -> 135 us  [shards(): lax.all_gather(weighted[h * half_rows:(h + 1) * half_rows], 'pz', axis=0,...]
    ppermute x6, waiting for transfers between devices: 61 us -> 1.69 us  [ring_shift(): lax.ppermute(value, axis, [(s, (s + shift) % size) for s in range(size)])]
    dot_general x4 -> x8, matrix products: 15.8 us -> 42.3 us  [shards(): lax.dot_general(block.reshape(row_count, points), column_half, (((1,), (1...]
    all_to_all x1, starting transfers between devices: 14.4 us -> 5.85 us  [shards(): lax.all_to_all(forces, PHASE, split_axis=2, concat_axis=1, tiled=True)]
  transfers between devices with their start and end apart: 10 -> 11, of which waited for: 6 -> 6; matrix products, arithmetic and copies ran while one was open for 7% -> 16% of each run, Pallas kernels for 0% -> 0%
where the time goes in v7:
time: 271 us; the launch traced here: 269 us
  waiting for transfers between devices  166 us (61%)
  matrix products  43.9 us (16%)
  starting transfers between devices  38.4 us (14%)
  between operations  13.8 us (5%)
  local copies, waits for them, and re-layouts  3.71 us (1%)
  other arithmetic  3.45 us (1%)
    all_gather x2, waiting for transfers between devices, shards(): lax.all_gather(weighted[h * half_rows:(h + 1) * half_rows], 'pz', axis=0,...  135 us
    dot_general x8, matrix products, shards(): lax.dot_general(block.reshape(row_count, points), column_half, (((1,), (1...  42.3 us
    ppermute x6, starting transfers between devices, ring_shift(): lax.ppermute(value, axis, [(s, (s + shift) % size) for s in range(size)])  22 us
    all_to_all x1, waiting for transfers between devices, shards(): lax.all_to_all(paired.transpose(1, 0, 2), ('sz', 'sy'), 0, 0, tiled=True)  14 us
    all_to_all x1, waiting for transfers between devices, shards(): lax.all_to_all(forces, PHASE, split_axis=2, concat_axis=1, tiled=True)  13.4 us
    all_to_all x1, starting transfers between devices, shards(): lax.all_to_all(paired.transpose(1, 0, 2), ('sz', 'sy'), 0, 0, tiled=True)  6.34 us
    all_to_all x1, starting transfers between devices, shards(): lax.all_to_all(forces, PHASE, split_axis=2, concat_axis=1, tiled=True)  5.85 us
  transfers between devices with their start and end apart: 11, of which 6 were waited for; matrix products, arithmetic and copies ran while one was open for 16% of the time, Pallas kernels for 0%

profile of v7, /device:TPU:1, one launch (start us, length us, event | category | flops | bytes accessed | tf_op | source)
XLA Modules:
  0.0 269.0 jit_solution(5195128049390468819)
XLA Ops:
  6.5 1.2 broadcast_multiply_fusion
  7.7 1.0 fusion.20
  8.7 0.0 all-gather.5.cloned.1.call-update
  8.8 0.0 all-gather.3.cloned.1.call-start
  8.8 4.0 %collective-permute-start = (f32[2,4,32,3072]{3,2,1,0:T(8,128)}, f32[2,4,32,3072]{3,2,1,0:T(8,128)}, u32[]{:S(2)}, u32[]{:S(2)}) collective-permute-start(f32[2,4,32,3072]{3,2,1,0:T(8,128)} %param.6), channel_id=1, source_target_pairs={{0,128},{128,256},{256,384},{384,0},{1,129},{129,257},{257,385},{3... | collective-permute-start | bytes 9437192 | tf_op jit(solution)/shard_map/ppermute | solution.py:26
  12.8 4.3 %collective-permute-start.2 = (f32[2,4,32,3072]{3,2,1,0:T(8,128)}, f32[2,4,32,3072]{3,2,1,0:T(8,128)}, u32[]{:S(2)}, u32[]{:S(2)}) collective-permute-start(f32[2,4,32,3072]{3,2,1,0:T(8,128)} %param.6), channel_id=1, source_target_pairs={{0,256},{128,384},{256,0},{384,128},{1,257},{129,385},{257,1},{385... | collective-permute-start | bytes 9437192 | tf_op jit(solution)/shard_map/ppermute | solution.py:26
  17.1 0.0 all-gather.3.cloned.1.call-update
  17.2 3.1 %collective-permute-start.4 = (f32[2,4,32,3072]{3,2,1,0:T(8,128)}, f32[2,4,32,3072]{3,2,1,0:T(8,128)}, u32[]{:S(2)}, u32[]{:S(2)}) collective-permute-start(f32[2,4,32,3072]{3,2,1,0:T(8,128)} %param.6), channel_id=1, source_target_pairs={{0,384},{128,0},{256,128},{384,256},{1,385},{129,1},{257,129},{385... | collective-permute-start | bytes 9437192 | tf_op jit(solution)/shard_map/ppermute | solution.py:26
  20.3 71.0 %all-gather.5.cloned.1.call-done = f32[128,3072]{1,0:T(8,128)} async-done(((f32[32,3072]{1,0:T(8,128)}), f32[128,3072]{1,0:T(8,128)}) %all-gather.5.cloned.1.call-update) | async-done | bytes 1572880 | tf_op jit(solution)/shard_map/all_gather | solution.py:36
  91.2 5.7 %fusion.22 = f32[128,256]{1,0:T(8,128)S(1)} fusion(f32[128,3072]{1,0:T(8,128)} %all-gather.5.cloned.1.call-done, f32[256,3072]{1,0:T(8,128)} %bitcast.4), kind=kOutput, calls=%fused_computation.43 | convolution fusion | flops 1207959552 | bytes 4849664 | tf_op jit(solution)/shard_map/dot_general | solution.py:47
  97.0 0.0 collective-permute-done
  97.0 5.1 %fusion.24 = f32[128,256]{1,0:T(8,128)S(1)} fusion(f32[128,3072]{1,0:T(8,128)S(1)} %copy-done, f32[256,3072]{1,0:T(8,128)} %bitcast.12), kind=kOutput, calls=%fused_computation.45 | convolution fusion | flops 1207959552 | bytes 4849664 | tf_op jit(solution)/shard_map/dot_general | solution.py:47
  102.1 64.2 %all-gather.3.cloned.1.call-done = f32[128,3072]{1,0:T(8,128)} async-done(((f32[32,3072]{1,0:T(8,128)}), f32[128,3072]{1,0:T(8,128)}) %all-gather.3.cloned.1.call-update) | async-done | bytes 1572880 | tf_op jit(solution)/shard_map/all_gather | solution.py:36
  166.3 5.7 %fusion.23 = f32[128,256]{1,0:T(8,128)S(1)} fusion(f32[128,3072]{1,0:T(8,128)} %all-gather.3.cloned.1.call-done, f32[256,3072]{1,0:T(8,128)} %bitcast.12), kind=kOutput, calls=%fused_computation.44 | convolution fusion | flops 1207959552 | bytes 4849664 | tf_op jit(solution)/shard_map/dot_general | solution.py:47
  172.1 5.5 %collective-permute-start.1 = (f32[256,256]{0,1:T(8,128)S(1)}, f32[256,256]{0,1:T(8,128)S(1)}, u32[]{:S(2)}, u32[]{:S(2)}) collective-permute-start(f32[256,256]{0,1:T(8,128)S(1)} %bitcast.127), channel_id=1, source_target_pairs={{0,384},{128,0},{256,128},{384,256},{1,385},{129,1},{257,129},{385... | collective-permute-start | bytes 786440 | tf_op jit(solution)/shard_map/ppermute | solution.py:26
  177.6 5.2 %fusion.25 = f32[128,256]{1,0:T(8,128)S(1)} fusion(f32[128,3072]{1,0:T(8,128)S(1)} %copy-done.1, f32[256,3072]{1,0:T(8,128)} %bitcast.21), kind=kOutput, calls=%fused_computation.46 | convolution fusion | flops 1207959552 | bytes 4849664 | tf_op jit(solution)/shard_map/dot_general | solution.py:47
  182.7 5.1 %fusion.26 = f32[128,256]{1,0:T(8,128)S(1)} fusion(f32[128,3072]{1,0:T(8,128)S(1)} %copy-done, f32[256,3072]{1,0:T(8,128)} %bitcast.21), kind=kOutput, calls=%fused_computation.47 | convolution fusion | flops 1207959552 | bytes 4849664 | tf_op jit(solution)/shard_map/dot_general | solution.py:47
  187.9 2.5 collective-permute-start.3
  190.4 5.2 %fusion.27 = f32[128,256]{1,0:T(8,128)S(1)} fusion(f32[128,3072]{1,0:T(8,128)S(1)} %copy-done.1, f32[256,3072]{1,0:T(8,128)} %bitcast.30), kind=kOutput, calls=%fused_computation.48 | convolution fusion | flops 1207959552 | bytes 4849664 | tf_op jit(solution)/shard_map/dot_general | solution.py:47
  195.6 5.1 %fusion.28 = f32[128,256]{1,0:T(8,128)S(1)} fusion(f32[128,3072]{1,0:T(8,128)S(1)} %copy-done, f32[256,3072]{1,0:T(8,128)} %bitcast.30), kind=kOutput, calls=%fused_computation.49 | convolution fusion | flops 1207959552 | bytes 4849664 | tf_op jit(solution)/shard_map/dot_general | solution.py:47
  200.7 2.7 %collective-permute-start.5 = (f32[256,256]{0,1:T(8,128)S(1)}, f32[256,256]{0,1:T(8,128)S(1)}, u32[]{:S(2)}, u32[]{:S(2)}) collective-permute-start(f32[256,256]{0,1:T(8,128)S(1)} %bitcast.129), channel_id=1, source_target_pairs={{0,128},{128,256},{256,384},{384,0},{1,129},{129,257},{257,385},{3... | collective-permute-start | bytes 786440 | tf_op jit(solution)/shard_map/ppermute | solution.py:26
  203.5 5.2 %fusion.21 = f32[128,256]{1,0:T(8,128)S(1)} fusion(f32[128,3072]{1,0:T(8,128)S(1)} %copy-done.1, f32[256,3072]{1,0:T(8,128)} %bitcast.4), kind=kOutput, calls=%fused_computation.42 | convolution fusion | flops 1207959552 | bytes 4849664 | tf_op jit(solution)/shard_map/dot_general | solution.py:47
  208.6 0.0 copy-start.2
  208.7 1.7 collective-permute-done.5
  210.4 0.1 pad_maximum_fusion
  210.5 0.4 copy.35
  210.9 0.6 convolution_bitcast_fusion
  211.5 0.4 copy.28
  211.9 0.1 select_bitcast_fusion
  212.0 4.1 %collective-permute-start.6 = (f32[256,16,32]{0,2,1:T(8,128)S(1)}, f32[256,16,32]{0,2,1:T(8,128)S(1)}, u32[]{:S(2)}, u32[]{:S(2)}) collective-permute-start(f32[256,16,32]{0,2,1:T(8,128)S(1)} %select_bitcast_fusion), channel_id=1, source_target_pairs={{0,1},{1,0},{2,3},{3,2},{4,5},{5,4},{6,7},{7,6},{8,9},{9,8},{10,11... | collective-permute-start | bytes 1572872 | tf_op jit(solution)/shard_map/ppermute | solution.py:78
  216.1 1.5 collective-permute-done.6
  217.6 0.9 fusion.2
  218.5 6.3 %all-to-all-start = ((f32[16,256,32]{1,2,0:T(8,128)}), f32[16,256,32]{1,2,0:T(8,128)S(1)}, u32[]{:S(2)}, u32[]{:S(2)}) async-start(f32[16,256,32]{1,2,0:T(8,128)} %fusion.2), calls=%async_computation | async-start | bytes 1048576 | tf_op jit(solution)/shard_map/all_to_all | solution.py:79
  224.9 0.1 fusion.9
  225.0 14.0 %all-to-all-done = f32[16,256,32]{1,2,0:T(8,128)S(1)} async-done(((f32[16,256,32]{1,2,0:T(8,128)}), f32[16,256,32]{1,2,0:T(8,128)S(1)}, u32[]{:S(2)}, u32[]{:S(2)}) %all-to-all-start) | async-done | bytes 524320 | tf_op jit(solution)/shard_map/all_to_all | solution.py:79
  239.0 0.1 reshape.91
  239.1 0.1 copy.30
  239.3 0.8 reshape.155
  240.0 5.8 %all-to-all-start.1 = ((f32[16,1,512]{2,1,0:T(1,128)}), f32[16,1,512]{2,1,0:T(1,128)S(1)}, u32[]{:S(2)}, u32[]{:S(2)}) async-start(f32[16,1,512]{2,1,0:T(1,128)} %reshape.155), calls=%async_computation.1 | async-start | bytes 65536 | tf_op jit(solution)/shard_map/all_to_all | solution.py:81
  245.9 0.1 fusion.11
  246.0 0.1 maximum_multiply_fusion
  246.1 13.4 %all-to-all-done.1 = f32[16,1,512]{2,1,0:T(1,128)S(1)} async-done(((f32[16,1,512]{2,1,0:T(1,128)}), f32[16,1,512]{2,1,0:T(1,128)S(1)}, u32[]{:S(2)}, u32[]{:S(2)}) %all-to-all-start.1) | async-done | bytes 32800 | tf_op jit(solution)/shard_map/all_to_all | solution.py:81
  259.6 0.5 broadcast.154
  260.1 0.7 reduce
  260.8 0.1 reshape.156
  261.0 0.1 reshape.92
  261.1 0.1 copy.33
  261.2 1.0 fusion.29
  (18 shorter events, 0.2 us)
Async XLA Ops:
  6.5 84.7 %all-gather.5.cloned.1.call-start = ((), (), s32[]{:S(2)}) async-start(), calls=%async_computation.3 | async-start | bytes 1966080 | tf_op jit(solution)/shard_map/all_gather | solution.py:36
  8.8 157.6 %all-gather.3.cloned.1.call-start = ((), (), s32[]{:S(2)}) async-start(), calls=%async_computation.2 | async-start | bytes 1966080 | tf_op jit(solution)/shard_map/all_gather | solution.py:36
  8.8 88.1 %collective-permute-start = (f32[2,4,32,3072]{3,2,1,0:T(8,128)}, f32[2,4,32,3072]{3,2,1,0:T(8,128)}, u32[]{:S(2)}, u32[]{:S(2)}) collective-permute-start(f32[2,4,32,3072]{3,2,1,0:T(8,128)} %param.6), channel_id=1, source_target_pairs={{0,128},{128,256},{256,384},{384,0},{1,129},{129,257},{257,385},{3... | collective-permute-start | bytes 9437192 | tf_op jit(solution)/shard_map/ppermute | solution.py:26
  12.8 164.8 %collective-permute-start.2 = (f32[2,4,32,3072]{3,2,1,0:T(8,128)}, f32[2,4,32,3072]{3,2,1,0:T(8,128)}, u32[]{:S(2)}, u32[]{:S(2)}) collective-permute-start(f32[2,4,32,3072]{3,2,1,0:T(8,128)} %param.6), channel_id=1, source_target_pairs={{0,256},{128,384},{256,0},{384,128},{1,257},{129,385},{257,1},{385... | collective-permute-start | bytes 9437192 | tf_op jit(solution)/shard_map/ppermute | solution.py:26
  17.2 173.2 %collective-permute-start.4 = (f32[2,4,32,3072]{3,2,1,0:T(8,128)}, f32[2,4,32,3072]{3,2,1,0:T(8,128)}, u32[]{:S(2)}, u32[]{:S(2)}) collective-permute-start(f32[2,4,32,3072]{3,2,1,0:T(8,128)} %param.6), channel_id=1, source_target_pairs={{0,384},{128,0},{256,128},{384,256},{1,385},{129,1},{257,129},{385... | collective-permute-start | bytes 9437192 | tf_op jit(solution)/shard_map/ppermute | solution.py:26
  91.2 5.7 %copy-start = (f32[128,3072]{1,0:T(8,128)S(1)}, f32[128,3072]{1,0:T(8,128)}, u32[]{:S(2)}) copy-start(f32[128,3072]{1,0:T(8,128)} %all-gather.5.cloned.1.call-done) | copy-start | bytes 4718596
  166.3 11.2 %copy-start.1 = (f32[128,3072]{1,0:T(8,128)S(1)}, f32[128,3072]{1,0:T(8,128)}, u32[]{:S(2)}) copy-start(f32[128,3072]{1,0:T(8,128)} %all-gather.3.cloned.1.call-done) | copy-start | bytes 4718596
  172.1 36.6 %collective-permute-start.1 = (f32[256,256]{0,1:T(8,128)S(1)}, f32[256,256]{0,1:T(8,128)S(1)}, u32[]{:S(2)}, u32[]{:S(2)}) collective-permute-start(f32[256,256]{0,1:T(8,128)S(1)} %bitcast.127), channel_id=1, source_target_pairs={{0,384},{128,0},{256,128},{384,256},{1,385},{129,1},{257,129},{385... | collective-permute-start | bytes 786440 | tf_op jit(solution)/shard_map/ppermute | solution.py:26
  187.9 20.8 %collective-permute-start.3 = (f32[256,256]{0,1:T(8,128)S(1)}, f32[256,256]{0,1:T(8,128)S(1)}, u32[]{:S(2)}, u32[]{:S(2)}) collective-permute-start(f32[256,256]{0,1:T(8,128)S(1)} %bitcast.128), channel_id=1, source_target_pairs={{0,256},{128,384},{256,0},{384,128},{1,257},{129,385},{257,1},{385... | collective-permute-start | bytes 786440 | tf_op jit(solution)/shard_map/ppermute | solution.py:26
  200.7 9.6 %collective-permute-start.5 = (f32[256,256]{0,1:T(8,128)S(1)}, f32[256,256]{0,1:T(8,128)S(1)}, u32[]{:S(2)}, u32[]{:S(2)}) collective-permute-start(f32[256,256]{0,1:T(8,128)S(1)} %bitcast.129), channel_id=1, source_target_pairs={{0,128},{128,256},{256,384},{384,0},{1,129},{129,257},{257,385},{3... | collective-permute-start | bytes 786440 | tf_op jit(solution)/shard_map/ppermute | solution.py:26
  208.6 2.3 copy-start.2
  212.0 5.6 %collective-permute-start.6 = (f32[256,16,32]{0,2,1:T(8,128)S(1)}, f32[256,16,32]{0,2,1:T(8,128)S(1)}, u32[]{:S(2)}, u32[]{:S(2)}) collective-permute-start(f32[256,16,32]{0,2,1:T(8,128)S(1)} %select_bitcast_fusion), channel_id=1, source_target_pairs={{0,1},{1,0},{2,3},{3,2},{4,5},{5,4},{6,7},{7,6},{8,9},{9,8},{10,11... | collective-permute-start | bytes 1572872 | tf_op jit(solution)/shard_map/ppermute | solution.py:78
  218.5 20.5 %all-to-all-start = ((f32[16,256,32]{1,2,0:T(8,128)}), f32[16,256,32]{1,2,0:T(8,128)S(1)}, u32[]{:S(2)}, u32[]{:S(2)}) async-start(f32[16,256,32]{1,2,0:T(8,128)} %fusion.2), calls=%async_computation | async-start | bytes 1048576 | tf_op jit(solution)/shard_map/all_to_all | solution.py:79
  240.0 19.5 %all-to-all-start.1 = ((f32[16,1,512]{2,1,0:T(1,128)}), f32[16,1,512]{2,1,0:T(1,128)S(1)}, u32[]{:S(2)}, u32[]{:S(2)}) async-start(f32[16,1,512]{2,1,0:T(1,128)} %reshape.155), calls=%async_computation.1 | async-start | bytes 65536 | tf_op jit(solution)/shard_map/all_to_all | solution.py:81
Sparse Core Ops, SparseCore 0:
  9.5 81.7 all-gather.4
  93.3 72.9 all-gather.2

commit v8 on v6

--- a/solution.py
+++ b/solution.py
@@ -29,9 +29,9 @@
 def shards(pressure, mode_shapes, point_weight, panel_order):
     nx = lax.axis_size("px")
     xi = lax.axis_index("px")
-    weighted = mode_shapes * point_weight[None, :]
-    column_modes = lax.all_gather(weighted, "pz", axis=0, tiled=True)
-    ring = [pressure] + [ring_shift(pressure, "px", nx, d) for d in range(1, nx)]
+    column_modes = lax.all_gather(mode_shapes, "pz", axis=0, tiled=True)
+    weighted = pressure * point_weight
+    ring = [weighted] + [ring_shift(weighted, "px", nx, d) for d in range(1, nx)]
     two, phase_dev, excite, points = pressure.shape
     row_count = two * phase_dev * excite
     pieces = []

time: 242 us -> 251 us (1.037)
  starting transfers between devices: 46.9 us -> 53.8 us
    ppermute x1, starting transfers between devices: 3.84 us -> 10.9 us  [shards(): paired = mine + lax.ppermute(other, 'sc', [(0, 1), (1, 0)])]
    all_gather x1, waiting for transfers between devices: 65 us -> 60.9 us  [shards(): column_modes = lax.all_gather(mode_shapes, 'pz', axis=0, tiled=True)]
    ppermute x6, waiting for transfers between devices: 61 us -> 64.8 us  [ring_shift(): lax.ppermute(value, axis, [(s, (s + shift) % size) for s in range(size)])]
  transfers between devices with their start and end apart: 10 -> 10, of which waited for: 6 -> 6; matrix products, arithmetic and copies ran while one was open for 7% -> 8% of each run, Pallas kernels for 0% -> 0%
where the time goes in v8:
time: 251 us; the launch traced here: 249 us
  waiting for transfers between devices  155 us (62%)
  starting transfers between devices  53.8 us (21%)
  matrix products  19.2 us (8%)
  between operations  13.7 us (5%)
  other arithmetic  4.47 us (2%)
  local copies, waits for them, and re-layouts  2.7 us (1%)
    ppermute x6, waiting for transfers between devices, ring_shift(): lax.ppermute(value, axis, [(s, (s + shift) % size) for s in range(size)])  64.8 us
    all_gather x1, waiting for transfers between devices, shards(): column_modes = lax.all_gather(mode_shapes, 'pz', axis=0, tiled=True)  60.9 us
    ppermute x6, starting transfers between devices, ring_shift(): lax.ppermute(value, axis, [(s, (s + shift) % size) for s in range(size)])  20.8 us
    dot_general x4, matrix products, shards(): lax.dot_general(block.reshape(row_count, points), column_modes, (((1,), (...  17.6 us
    all_to_all x1, waiting for transfers between devices, shards(): lax.all_to_all(paired.transpose(1, 0, 2), ('sz', 'sy'), 0, 0, tiled=True)  14 us
    all_to_all x1, waiting for transfers between devices, shards(): lax.all_to_all(forces, PHASE, split_axis=2, concat_axis=1, tiled=True)  13.4 us
    all_to_all x1, starting transfers between devices, shards(): lax.all_to_all(forces, PHASE, split_axis=2, concat_axis=1, tiled=True)  13.1 us
    ppermute x1, starting transfers between devices, shards(): paired = mine + lax.ppermute(other, 'sc', [(0, 1), (1, 0)])  10.9 us
  transfers between devices with their start and end apart: 10, of which 6 were waited for; matrix products, arithmetic and copies ran while one was open for 8% of the time, Pallas kernels for 0%

profile of v8, /device:TPU:1, one launch (start us, length us, event | category | flops | bytes accessed | tf_op | source)
XLA Modules:
  0.0 249.1 jit_solution(3561024107117879027)
XLA Ops:
  6.5 0.0 all-gather.2.cloned.1.call-start
  6.5 0.7 all-gather.2.cloned.1.call-update
  7.3 2.3 broadcast_multiply_fusion
  9.6 5.2 %collective-permute-start.4 = (f32[2,4,32,3072]{3,2,1,0:T(8,128)S(1)}, f32[2,4,32,3072]{3,2,1,0:T(8,128)}, u32[]{:S(2)}, u32[]{:S(2)}) collective-permute-start(f32[2,4,32,3072]{3,2,1,0:T(8,128)S(1)} %broadcast_multiply_fusion), channel_id=1, source_target_pairs={{0,384},{128,0},{256,128},{384,256},{1,385},{129,1},{257,129},{385... | collective-permute-start | bytes 9437192 | tf_op jit(solution)/shard_map/ppermute | solution.py:26
  14.8 1.9 collective-permute-start
  16.7 3.6 %collective-permute-start.2 = (f32[2,4,32,3072]{3,2,1,0:T(8,128)S(1)}, f32[2,4,32,3072]{3,2,1,0:T(8,128)}, u32[]{:S(2)}, u32[]{:S(2)}) collective-permute-start(f32[2,4,32,3072]{3,2,1,0:T(8,128)S(1)} %broadcast_multiply_fusion), channel_id=1, source_target_pairs={{0,256},{128,384},{256,0},{384,128},{1,257},{129,385},{257,1},{385... | collective-permute-start | bytes 9437192 | tf_op jit(solution)/shard_map/ppermute | solution.py:26
  20.4 62.5 %collective-permute-done.4 = f32[2,4,32,3072]{3,2,1,0:T(8,128)} collective-permute-done((f32[2,4,32,3072]{3,2,1,0:T(8,128)S(1)}, f32[2,4,32,3072]{3,2,1,0:T(8,128)}, u32[]{:S(2)}, u32[]{:S(2)}) %collective-permute-start.4) | collective-permute-done | bytes 3145760 | tf_op jit(solution)/shard_map/ppermute | solution.py:26
  82.9 60.9 %all-gather.2.cloned.1.call-done = f32[256,3072]{1,0:T(8,128)} async-done(((f32[64,3072]{1,0:T(8,128)}), f32[256,3072]{1,0:T(8,128)}) %all-gather.2.cloned.1.call-update) | async-done | bytes 3145744 | tf_op jit(solution)/shard_map/all_gather | solution.py:32
  143.8 0.0 copy-start
  143.8 5.7 %fusion.22 = f32[256,256]{0,1:T(8,128)S(1)} fusion(f32[256,3072]{1,0:T(8,128)} %bitcast.10, f32[256,3072]{1,0:T(8,128)} %all-gather.2.cloned.1.call-done), kind=kOutput, calls=%fused_computation.40 | convolution fusion | flops 2415919104 | bytes 6553600 | tf_op jit(solution)/shard_map/dot_general | solution.py:39
  149.5 3.1 %collective-permute-start.5 = (f32[256,256]{0,1:T(8,128)S(1)}, f32[256,256]{0,1:T(8,128)S(1)}, u32[]{:S(2)}, u32[]{:S(2)}) collective-permute-start(f32[256,256]{0,1:T(8,128)S(1)} %fusion.22), channel_id=1, source_target_pairs={{0,128},{128,256},{256,384},{384,0},{1,129},{129,257},{257,385},{3... | collective-permute-start | bytes 786440 | tf_op jit(solution)/shard_map/ppermute | solution.py:26
  152.6 0.0 collective-permute-done
  152.6 0.0 copy-done
  152.6 4.6 %fusion.20 = f32[256,256]{0,1:T(8,128)S(1)} fusion(f32[256,3072]{1,0:T(8,128)} %bitcast.6, f32[256,3072]{1,0:T(8,128)S(1)} %copy-done), kind=kOutput, calls=%fused_computation.38 | convolution fusion | flops 2415919104 | bytes 6553600 | tf_op jit(solution)/shard_map/dot_general | solution.py:39
  157.2 3.4 %collective-permute-start.1 = (f32[256,256]{0,1:T(8,128)S(1)}, f32[256,256]{0,1:T(8,128)S(1)}, u32[]{:S(2)}, u32[]{:S(2)}) collective-permute-start(f32[256,256]{0,1:T(8,128)S(1)} %fusion.20), channel_id=1, source_target_pairs={{0,384},{128,0},{256,128},{384,256},{1,385},{129,1},{257,129},{385... | collective-permute-start | bytes 786440 | tf_op jit(solution)/shard_map/ppermute | solution.py:26
  160.6 0.0 collective-permute-done.2
  160.6 4.6 %fusion.21 = f32[256,256]{0,1:T(8,128)S(1)} fusion(f32[256,3072]{1,0:T(8,128)} %bitcast.8, f32[256,3072]{1,0:T(8,128)S(1)} %copy-done), kind=kOutput, calls=%fused_computation.39 | convolution fusion | flops 2415919104 | bytes 6553600 | tf_op jit(solution)/shard_map/dot_general | solution.py:39
  165.3 3.6 %collective-permute-start.3 = (f32[256,256]{0,1:T(8,128)S(1)}, f32[256,256]{0,1:T(8,128)S(1)}, u32[]{:S(2)}, u32[]{:S(2)}) collective-permute-start(f32[256,256]{0,1:T(8,128)S(1)} %fusion.21), channel_id=1, source_target_pairs={{0,256},{128,384},{256,0},{384,128},{1,257},{129,385},{257,1},{385... | collective-permute-start | bytes 786440 | tf_op jit(solution)/shard_map/ppermute | solution.py:26
  168.8 2.7 %convolution_bitcast_fusion.1 = f32[256,1,256]{0,2,1:T(8,128)S(1)} fusion(f32[256,3072]{1,0:T(8,128)S(1)} %bitcast.61, f32[256,3072]{1,0:T(8,128)S(1)} %copy-done), kind=kOutput, calls=%fused_computation.2 | convolution fusion | flops 2415919104 | bytes 6553600 | tf_op jit(solution)/shard_map/dot_general | solution.py:39
  171.6 0.0 copy-start.1
  171.6 0.0 collective-permute-done.5
  171.6 0.0 collective-permute-done.1
  171.6 2.3 collective-permute-done.3
  173.9 0.1 pad_maximum_fusion
  174.0 0.4 copy.21
  174.4 0.0 copy-done.1
  174.4 0.6 convolution_bitcast_fusion
  175.0 0.4 copy.22
  175.4 0.1 select_bitcast_fusion
  175.5 10.9 %collective-permute-start.6 = (f32[256,16,32]{0,2,1:T(8,128)S(1)}, f32[256,16,32]{0,2,1:T(8,128)S(1)}, u32[]{:S(2)}, u32[]{:S(2)}) collective-permute-start(f32[256,16,32]{0,2,1:T(8,128)S(1)} %select_bitcast_fusion), channel_id=1, source_target_pairs={{0,1},{1,0},{2,3},{3,2},{4,5},{5,4},{6,7},{7,6},{8,9},{9,8},{10,11... | collective-permute-start | bytes 1572872 | tf_op jit(solution)/shard_map/ppermute | solution.py:66
  186.4 1.5 collective-permute-done.6
  187.9 0.9 fusion.2
  188.8 8.9 %all-to-all-start = ((f32[16,256,32]{1,2,0:T(8,128)}), f32[16,256,32]{1,2,0:T(8,128)S(1)}, u32[]{:S(2)}, u32[]{:S(2)}) async-start(f32[16,256,32]{1,2,0:T(8,128)} %fusion.2), calls=%async_computation | async-start | bytes 1048576 | tf_op jit(solution)/shard_map/all_to_all | solution.py:67
  197.7 0.1 fusion.9
  197.8 14.0 %all-to-all-done = f32[16,256,32]{1,2,0:T(8,128)S(1)} async-done(((f32[16,256,32]{1,2,0:T(8,128)}), f32[16,256,32]{1,2,0:T(8,128)S(1)}, u32[]{:S(2)}, u32[]{:S(2)}) %all-to-all-start) | async-done | bytes 524320 | tf_op jit(solution)/shard_map/all_to_all | solution.py:67
  211.8 0.1 reshape.75
  212.0 0.1 copy.24
  212.1 0.8 reshape.139
  212.9 13.1 %all-to-all-start.1 = ((f32[16,1,512]{2,1,0:T(1,128)}), f32[16,1,512]{2,1,0:T(1,128)S(1)}, u32[]{:S(2)}, u32[]{:S(2)}) async-start(f32[16,1,512]{2,1,0:T(1,128)} %reshape.139), calls=%async_computation.1 | async-start | bytes 65536 | tf_op jit(solution)/shard_map/all_to_all | solution.py:69
  226.0 0.1 fusion.11
  226.2 0.1 maximum_multiply_fusion
  226.2 13.4 %all-to-all-done.1 = f32[16,1,512]{2,1,0:T(1,128)S(1)} async-done(((f32[16,1,512]{2,1,0:T(1,128)}), f32[16,1,512]{2,1,0:T(1,128)S(1)}, u32[]{:S(2)}, u32[]{:S(2)}) %all-to-all-start.1) | async-done | bytes 32800 | tf_op jit(solution)/shard_map/all_to_all | solution.py:69
  239.7 0.5 broadcast.154
  240.2 0.7 reduce
  240.9 0.1 reshape.140
  241.1 0.1 reshape.76
  241.3 0.1 copy.27
  241.3 1.0 fusion.23
  (4 shorter events, 0.1 us)
Async XLA Ops:
  6.5 137.3 %all-gather.2.cloned.1.call-start = ((), (), s32[]{:S(2)}) async-start(), calls=%async_computation.2 | async-start | bytes 3932160 | tf_op jit(solution)/shard_map/all_gather | solution.py:32
  9.6 73.3 %collective-permute-start.4 = (f32[2,4,32,3072]{3,2,1,0:T(8,128)S(1)}, f32[2,4,32,3072]{3,2,1,0:T(8,128)}, u32[]{:S(2)}, u32[]{:S(2)}) collective-permute-start(f32[2,4,32,3072]{3,2,1,0:T(8,128)S(1)} %broadcast_multiply_fusion), channel_id=1, source_target_pairs={{0,384},{128,0},{256,128},{384,256},{1,385},{129,1},{257,129},{385... | collective-permute-start | bytes 9437192 | tf_op jit(solution)/shard_map/ppermute | solution.py:26
  14.8 137.8 %collective-permute-start = (f32[2,4,32,3072]{3,2,1,0:T(8,128)S(1)}, f32[2,4,32,3072]{3,2,1,0:T(8,128)}, u32[]{:S(2)}, u32[]{:S(2)}) collective-permute-start(f32[2,4,32,3072]{3,2,1,0:T(8,128)S(1)} %broadcast_multiply_fusion), channel_id=1, source_target_pairs={{0,128},{128,256},{256,384},{384,0},{1,129},{129,257},{257,385},{3... | collective-permute-start | bytes 9437192 | tf_op jit(solution)/shard_map/ppermute | solution.py:26
  16.7 143.9 %collective-permute-start.2 = (f32[2,4,32,3072]{3,2,1,0:T(8,128)S(1)}, f32[2,4,32,3072]{3,2,1,0:T(8,128)}, u32[]{:S(2)}, u32[]{:S(2)}) collective-permute-start(f32[2,4,32,3072]{3,2,1,0:T(8,128)S(1)} %broadcast_multiply_fusion), channel_id=1, source_target_pairs={{0,256},{128,384},{256,0},{384,128},{1,257},{129,385},{257,1},{385... | collective-permute-start | bytes 9437192 | tf_op jit(solution)/shard_map/ppermute | solution.py:26
  143.8 8.8 %copy-start = (f32[256,3072]{1,0:T(8,128)S(1)}, f32[256,3072]{1,0:T(8,128)}, u32[]{:S(2)}) copy-start(f32[256,3072]{1,0:T(8,128)} %all-gather.2.cloned.1.call-done) | copy-start | bytes 9437188
  149.5 22.1 %collective-permute-start.5 = (f32[256,256]{0,1:T(8,128)S(1)}, f32[256,256]{0,1:T(8,128)S(1)}, u32[]{:S(2)}, u32[]{:S(2)}) collective-permute-start(f32[256,256]{0,1:T(8,128)S(1)} %fusion.22), channel_id=1, source_target_pairs={{0,128},{128,256},{256,384},{384,0},{1,129},{129,257},{257,385},{3... | collective-permute-start | bytes 786440 | tf_op jit(solution)/shard_map/ppermute | solution.py:26
  157.2 14.4 %collective-permute-start.1 = (f32[256,256]{0,1:T(8,128)S(1)}, f32[256,256]{0,1:T(8,128)S(1)}, u32[]{:S(2)}, u32[]{:S(2)}) collective-permute-start(f32[256,256]{0,1:T(8,128)S(1)} %fusion.20), channel_id=1, source_target_pairs={{0,384},{128,0},{256,128},{384,256},{1,385},{129,1},{257,129},{385... | collective-permute-start | bytes 786440 | tf_op jit(solution)/shard_map/ppermute | solution.py:26
  165.3 8.6 %collective-permute-start.3 = (f32[256,256]{0,1:T(8,128)S(1)}, f32[256,256]{0,1:T(8,128)S(1)}, u32[]{:S(2)}, u32[]{:S(2)}) collective-permute-start(f32[256,256]{0,1:T(8,128)S(1)} %fusion.21), channel_id=1, source_target_pairs={{0,256},{128,384},{256,0},{384,128},{1,257},{129,385},{257,1},{385... | collective-permute-start | bytes 786440 | tf_op jit(solution)/shard_map/ppermute | solution.py:26
  171.6 2.8 %copy-start.1 = (s32[8]{0:T(128)S(1)}, s32[8]{0:T(128)}, u32[]{:S(2)}) copy-start(s32[8]{0:T(128)} %param.9) | copy-start | bytes 100
  175.5 12.4 %collective-permute-start.6 = (f32[256,16,32]{0,2,1:T(8,128)S(1)}, f32[256,16,32]{0,2,1:T(8,128)S(1)}, u32[]{:S(2)}, u32[]{:S(2)}) collective-permute-start(f32[256,16,32]{0,2,1:T(8,128)S(1)} %select_bitcast_fusion), channel_id=1, source_target_pairs={{0,1},{1,0},{2,3},{3,2},{4,5},{5,4},{6,7},{7,6},{8,9},{9,8},{10,11... | collective-permute-start | bytes 1572872 | tf_op jit(solution)/shard_map/ppermute | solution.py:66
  188.8 23.0 %all-to-all-start = ((f32[16,256,32]{1,2,0:T(8,128)}), f32[16,256,32]{1,2,0:T(8,128)S(1)}, u32[]{:S(2)}, u32[]{:S(2)}) async-start(f32[16,256,32]{1,2,0:T(8,128)} %fusion.2), calls=%async_computation | async-start | bytes 1048576 | tf_op jit(solution)/shard_map/all_to_all | solution.py:67
  212.9 26.8 %all-to-all-start.1 = ((f32[16,1,512]{2,1,0:T(1,128)}), f32[16,1,512]{2,1,0:T(1,128)S(1)}, u32[]{:S(2)}, u32[]{:S(2)}) async-start(f32[16,1,512]{2,1,0:T(1,128)} %reshape.139), calls=%async_computation.1 | async-start | bytes 65536 | tf_op jit(solution)/shard_map/all_to_all | solution.py:69
Sparse Core Ops, SparseCore 0:
  9.5 134.3 all-gather.1

commit v9 on v6

--- a/solution.py
+++ b/solution.py
@@ -43,13 +43,12 @@
             precision=lax.Precision.HIGHEST,
             preferred_element_type=jnp.float32,
         )
-        pieces.append(partial if d == 0 else ring_shift(partial, "px", nx, -d))
-    own = jnp.stack(pieces, axis=1)
+        pieces.append(partial)
+    by_owner = jnp.take(jnp.stack(pieces), (xi - jnp.arange(nx)) % nx, axis=0)
+    own = lax.all_to_all(by_owner, "px", 0, 0, tiled=True).transpose(1, 0, 2)
     panel_count = panel_order.shape[0]
-    local_panels = panel_count // nx
     own = own.reshape(row_count, panel_count, -1)
-    slot = jnp.arange(panel_count, dtype=jnp.int32)
-    stored = ((xi + slot // local_panels) % nx) * local_panels + slot % local_panels
+    stored = jnp.arange(panel_count, dtype=jnp.int32)
     selector = (panel_order[:, None] == stored[None, :]).astype(jnp.float32)
     reordered = jnp.einsum(
         "rqc,pq->rpc", own, selector, precision=lax.Precision.HIGHEST

time: 242 us -> 254 us (1.050)
  waiting for transfers between devices: 155 us -> 164 us
    ppermute x6 -> x3, starting transfers between devices: 22.1 us -> 10.2 us  [ring_shift(): lax.ppermute(value, axis, [(s, (s + shift) % size) for s in range(size)])]
    all_to_all x0 -> x1, waiting for transfers between devices: none -> 9.52 us  [shards(): own = lax.all_to_all(by_owner, 'px', 0, 0, tiled=True).transpose(1, 0, 2)]
    ppermute x1, starting transfers between devices: 3.84 us -> 9.88 us  [shards(): paired = mine + lax.ppermute(other, 'sc', [(0, 1), (1, 0)])]
    all_to_all x1, starting transfers between devices: 6.59 us -> 11.7 us  [shards(): lax.all_to_all(paired.transpose(1, 0, 2), ('sz', 'sy'), 0, 0, tiled=True)]
    all_to_all x0 -> x1, starting transfers between devices: none -> 3.7 us  [shards(): own = lax.all_to_all(by_owner, 'px', 0, 0, tiled=True).transpose(1, 0, 2)]
    all_gather x1, waiting for transfers between devices: 65 us -> 61.5 us  [shards(): column_modes = lax.all_gather(weighted, 'pz', axis=0, tiled=True)]
    ppermute x6 -> x3, waiting for transfers between devices: 61 us -> 64.2 us  [ring_shift(): lax.ppermute(value, axis, [(s, (s + shift) % size) for s in range(size)])]
  transfers between devices with their start and end apart: 10 -> 8, of which waited for: 6 -> 7; matrix products, arithmetic and copies ran while one was open for 7% -> 4% of each run, Pallas kernels for 0% -> 0%
where the time goes in v9:
time: 254 us; the launch traced here: 252 us
  waiting for transfers between devices  164 us (65%)
  starting transfers between devices  48.3 us (19%)
  matrix products  17.4 us (7%)
  between operations  13.7 us (5%)
  other arithmetic  5.38 us (2%)
  local copies, waits for them, and re-layouts  3.31 us (1%)
    ppermute x3, waiting for transfers between devices, ring_shift(): lax.ppermute(value, axis, [(s, (s + shift) % size) for s in range(size)])  64.2 us
    all_gather x1, waiting for transfers between devices, shards(): column_modes = lax.all_gather(weighted, 'pz', axis=0, tiled=True)  61.5 us
    dot_general x4, matrix products, shards(): lax.dot_general(block.reshape(row_count, points), column_modes, (((1,), (...  15.8 us
    all_to_all x1, waiting for transfers between devices, shards(): lax.all_to_all(paired.transpose(1, 0, 2), ('sz', 'sy'), 0, 0, tiled=True)  14 us
    all_to_all x1, waiting for transfers between devices, shards(): lax.all_to_all(forces, PHASE, split_axis=2, concat_axis=1, tiled=True)  13.4 us
    all_to_all x1, starting transfers between devices, shards(): lax.all_to_all(forces, PHASE, split_axis=2, concat_axis=1, tiled=True)  12.8 us
    all_to_all x1, starting transfers between devices, shards(): lax.all_to_all(paired.transpose(1, 0, 2), ('sz', 'sy'), 0, 0, tiled=True)  11.7 us
    ppermute x3, starting transfers between devices, ring_shift(): lax.ppermute(value, axis, [(s, (s + shift) % size) for s in range(size)])  10.2 us
  transfers between devices with their start and end apart: 8, of which 7 were waited for; matrix products, arithmetic and copies ran while one was open for 4% of the time, Pallas kernels for 0%

profile of v9, /device:TPU:1, one launch (start us, length us, event | category | flops | bytes accessed | tf_op | source)
XLA Modules:
  0.0 252.1 jit_solution(11691357328711039169)
XLA Ops:
  6.5 0.0 all-gather.2.cloned.1.call-start
  6.5 2.1 broadcast_multiply_fusion
  8.6 0.0 all-gather.2.cloned.1.call-update
  8.6 5.2 %collective-permute-start.2 = (f32[2,4,32,3072]{3,2,1,0:T(8,128)}, f32[2,4,32,3072]{3,2,1,0:T(8,128)}, u32[]{:S(2)}, u32[]{:S(2)}) collective-permute-start(f32[2,4,32,3072]{3,2,1,0:T(8,128)} %param.6), channel_id=1, source_target_pairs={{0,384},{128,0},{256,128},{384,256},{1,385},{129,1},{257,129},{385... | collective-permute-start | bytes 9437192 | tf_op jit(solution)/shard_map/ppermute | solution.py:26
  13.9 2.4 collective-permute-start.1
  16.3 2.5 collective-permute-start
  18.9 63.4 %collective-permute-done.2 = f32[2,4,32,3072]{3,2,1,0:T(8,128)} collective-permute-done((f32[2,4,32,3072]{3,2,1,0:T(8,128)}, f32[2,4,32,3072]{3,2,1,0:T(8,128)}, u32[]{:S(2)}, u32[]{:S(2)}) %collective-permute-start.2) | collective-permute-done | bytes 3145760 | tf_op jit(solution)/shard_map/ppermute | solution.py:26
  82.3 61.5 %all-gather.2.cloned.1.call-done = f32[256,3072]{1,0:T(8,128)} async-done(((f32[64,3072]{1,0:T(8,128)}), f32[256,3072]{1,0:T(8,128)}) %all-gather.2.cloned.1.call-update) | async-done | bytes 3145744 | tf_op jit(solution)/shard_map/all_gather | solution.py:33
  143.8 0.0 copy-start
  143.8 5.7 %convolution_bitcast_fusion.1 = f32[1,256,256]{1,2,0:T(8,128)S(1)} fusion(f32[256,3072]{1,0:T(8,128)} %all-gather.2.cloned.1.call-done, f32[256,3072]{1,0:T(8,128)} %bitcast.13), kind=kOutput, calls=%fused_computation.2 | convolution fusion | flops 2415919104 | bytes 6553600 | tf_op jit(solution)/shard_map/dot_general | solution.py:39
  149.5 0.0 collective-permute-done.1
  149.5 0.0 copy-done
  149.5 4.7 %convolution_bitcast_fusion.2 = f32[1,256,256]{1,2,0:T(8,128)S(1)} fusion(f32[256,3072]{1,0:T(8,128)S(1)} %copy-done, f32[256,3072]{1,0:T(8,128)} %bitcast.10), kind=kOutput, calls=%fused_computation.3 | convolution fusion | flops 2415919104 | bytes 6553600 | tf_op jit(solution)/shard_map/dot_general | solution.py:39
  154.2 0.8 collective-permute-done
  154.9 0.0 copy-start.1
  154.9 2.7 %convolution_bitcast_fusion.3 = f32[1,256,256]{1,2,0:T(8,128)S(1)} fusion(f32[256,3072]{1,0:T(8,128)S(1)} %copy-done, f32[256,3072]{1,0:T(8,128)S(1)} %bitcast.80), kind=kOutput, calls=%fused_computation.4 | convolution fusion | flops 2415919104 | bytes 6553600 | tf_op jit(solution)/shard_map/dot_general | solution.py:39
  157.7 0.0 copy-done.1
  157.7 2.7 %convolution_bitcast_fusion.4 = f32[1,256,256]{1,2,0:T(8,128)S(1)} fusion(f32[256,3072]{1,0:T(8,128)S(1)} %copy-done, f32[256,3072]{1,0:T(8,128)S(1)} %bitcast.79), kind=kOutput, calls=%fused_computation.5 | convolution fusion | flops 2415919104 | bytes 6553600 | tf_op jit(solution)/shard_map/dot_general | solution.py:39
  160.4 0.1 pad_maximum_fusion
  160.5 0.6 gather_fusion
  161.1 0.0 copy-start.2
  161.1 1.1 broadcast_select_fusion
  162.2 3.7 %all-to-all-start = ((f32[4,256,256]{1,2,0:T(8,128)}), f32[4,256,256]{1,2,0:T(8,128)S(1)}, u32[]{:S(2)}, u32[]{:S(2)}) async-start(f32[4,256,256]{1,2,0:T(8,128)} %broadcast_select_fusion), calls=%async_computation | async-start | bytes 2097152 | tf_op jit(solution)/shard_map/all_to_all | solution.py:48
  166.0 9.5 %all-to-all-done = f32[4,256,256]{1,2,0:T(8,128)S(1)} async-done(((f32[4,256,256]{1,2,0:T(8,128)}), f32[4,256,256]{1,2,0:T(8,128)S(1)}, u32[]{:S(2)}, u32[]{:S(2)}) %all-to-all-start) | async-done | bytes 1048608 | tf_op jit(solution)/shard_map/all_to_all | solution.py:48
  175.5 0.4 copy.12
  175.9 0.0 copy-done.2
  175.9 0.6 convolution_bitcast_fusion
  176.5 0.4 copy.13
  176.9 0.1 select_bitcast_fusion
  177.0 9.9 %collective-permute-start.3 = (f32[256,16,32]{0,2,1:T(8,128)S(1)}, f32[256,16,32]{0,2,1:T(8,128)S(1)}, u32[]{:S(2)}, u32[]{:S(2)}) collective-permute-start(f32[256,16,32]{0,2,1:T(8,128)S(1)} %select_bitcast_fusion), channel_id=1, source_target_pairs={{0,1},{1,0},{2,3},{3,2},{4,5},{5,4},{6,7},{7,6},{8,9},{9,8},{10,11... | collective-permute-start | bytes 1572872 | tf_op jit(solution)/shard_map/ppermute | solution.py:65
  186.9 1.5 collective-permute-done.3
  188.4 0.9 fusion.2
  189.3 11.7 %all-to-all-start.1 = ((f32[16,256,32]{1,2,0:T(8,128)}), f32[16,256,32]{1,2,0:T(8,128)S(1)}, u32[]{:S(2)}, u32[]{:S(2)}) async-start(f32[16,256,32]{1,2,0:T(8,128)} %fusion.2), calls=%async_computation.1 | async-start | bytes 1048576 | tf_op jit(solution)/shard_map/all_to_all | solution.py:66
  201.0 0.1 fusion.9
  201.1 14.0 %all-to-all-done.1 = f32[16,256,32]{1,2,0:T(8,128)S(1)} async-done(((f32[16,256,32]{1,2,0:T(8,128)}), f32[16,256,32]{1,2,0:T(8,128)S(1)}, u32[]{:S(2)}, u32[]{:S(2)}) %all-to-all-start.1) | async-done | bytes 524320 | tf_op jit(solution)/shard_map/all_to_all | solution.py:66
  215.1 0.1 reshape.95
  215.3 0.1 copy.15
  215.4 0.8 reshape.167
  216.1 12.8 %all-to-all-start.2 = ((f32[16,1,512]{2,1,0:T(1,128)}), f32[16,1,512]{2,1,0:T(1,128)S(1)}, u32[]{:S(2)}, u32[]{:S(2)}) async-start(f32[16,1,512]{2,1,0:T(1,128)} %reshape.167), calls=%async_computation.2 | async-start | bytes 65536 | tf_op jit(solution)/shard_map/all_to_all | solution.py:68
  229.0 0.1 fusion.11
  229.1 0.1 maximum_multiply_fusion
  229.2 13.4 %all-to-all-done.2 = f32[16,1,512]{2,1,0:T(1,128)S(1)} async-done(((f32[16,1,512]{2,1,0:T(1,128)}), f32[16,1,512]{2,1,0:T(1,128)S(1)}, u32[]{:S(2)}, u32[]{:S(2)}) %all-to-all-start.2) | async-done | bytes 32800 | tf_op jit(solution)/shard_map/all_to_all | solution.py:68
  242.7 0.5 broadcast.166
  243.2 0.7 reduce
  243.9 0.1 reshape.168
  244.1 0.1 reshape.96
  244.2 0.1 copy.18
  244.3 1.0 fusion.18
  (6 shorter events, 0.1 us)
Async XLA Ops:
  6.5 137.3 %all-gather.2.cloned.1.call-start = ((), (), s32[]{:S(2)}) async-start(), calls=%async_computation.3 | async-start | bytes 3932160 | tf_op jit(solution)/shard_map/all_gather | solution.py:33
  8.6 73.6 %collective-permute-start.2 = (f32[2,4,32,3072]{3,2,1,0:T(8,128)}, f32[2,4,32,3072]{3,2,1,0:T(8,128)}, u32[]{:S(2)}, u32[]{:S(2)}) collective-permute-start(f32[2,4,32,3072]{3,2,1,0:T(8,128)} %param.6), channel_id=1, source_target_pairs={{0,384},{128,0},{256,128},{384,256},{1,385},{129,1},{257,129},{385... | collective-permute-start | bytes 9437192 | tf_op jit(solution)/shard_map/ppermute | solution.py:26
  13.9 135.6 %collective-permute-start.1 = (f32[2,4,32,3072]{3,2,1,0:T(8,128)}, f32[2,4,32,3072]{3,2,1,0:T(8,128)}, u32[]{:S(2)}, u32[]{:S(2)}) collective-permute-start(f32[2,4,32,3072]{3,2,1,0:T(8,128)} %param.6), channel_id=1, source_target_pairs={{0,256},{128,384},{256,0},{384,128},{1,257},{129,385},{257,1},{385... | collective-permute-start | bytes 9437192 | tf_op jit(solution)/shard_map/ppermute | solution.py:26
  16.3 138.6 %collective-permute-start = (f32[2,4,32,3072]{3,2,1,0:T(8,128)}, f32[2,4,32,3072]{3,2,1,0:T(8,128)S(1)}, u32[]{:S(2)}, u32[]{:S(2)}) collective-permute-start(f32[2,4,32,3072]{3,2,1,0:T(8,128)} %param.6), channel_id=1, source_target_pairs={{0,128},{128,256},{256,384},{384,0},{1,129},{129,257},{257,385},{3... | collective-permute-start | bytes 9437192 | tf_op jit(solution)/shard_map/ppermute | solution.py:26
  143.8 5.7 %copy-start = (f32[256,3072]{1,0:T(8,128)S(1)}, f32[256,3072]{1,0:T(8,128)}, u32[]{:S(2)}) copy-start(f32[256,3072]{1,0:T(8,128)} %all-gather.2.cloned.1.call-done) | copy-start | bytes 9437188
  154.9 2.7 %copy-start.1 = (f32[2,4,32,3072]{3,2,1,0:T(8,128)S(1)}, f32[2,4,32,3072]{3,2,1,0:T(8,128)}, u32[]{:S(2)}) copy-start(f32[2,4,32,3072]{3,2,1,0:T(8,128)} %param.6) | copy-start | bytes 9437188
  161.1 14.8 %copy-start.2 = (s32[8]{0:T(128)S(1)}, s32[8]{0:T(128)}, u32[]{:S(2)}) copy-start(s32[8]{0:T(128)} %param.9) | copy-start | bytes 100
  162.2 13.2 %all-to-all-start = ((f32[4,256,256]{1,2,0:T(8,128)}), f32[4,256,256]{1,2,0:T(8,128)S(1)}, u32[]{:S(2)}, u32[]{:S(2)}) async-start(f32[4,256,256]{1,2,0:T(8,128)} %broadcast_select_fusion), calls=%async_computation | async-start | bytes 2097152 | tf_op jit(solution)/shard_map/all_to_all | solution.py:48
  177.0 11.4 %collective-permute-start.3 = (f32[256,16,32]{0,2,1:T(8,128)S(1)}, f32[256,16,32]{0,2,1:T(8,128)S(1)}, u32[]{:S(2)}, u32[]{:S(2)}) collective-permute-start(f32[256,16,32]{0,2,1:T(8,128)S(1)} %select_bitcast_fusion), channel_id=1, source_target_pairs={{0,1},{1,0},{2,3},{3,2},{4,5},{5,4},{6,7},{7,6},{8,9},{9,8},{10,11... | collective-permute-start | bytes 1572872 | tf_op jit(solution)/shard_map/ppermute | solution.py:65
  189.3 25.8 %all-to-all-start.1 = ((f32[16,256,32]{1,2,0:T(8,128)}), f32[16,256,32]{1,2,0:T(8,128)S(1)}, u32[]{:S(2)}, u32[]{:S(2)}) async-start(f32[16,256,32]{1,2,0:T(8,128)} %fusion.2), calls=%async_computation.1 | async-start | bytes 1048576 | tf_op jit(solution)/shard_map/all_to_all | solution.py:66
  216.1 26.5 %all-to-all-start.2 = ((f32[16,1,512]{2,1,0:T(1,128)}), f32[16,1,512]{2,1,0:T(1,128)S(1)}, u32[]{:S(2)}, u32[]{:S(2)}) async-start(f32[16,1,512]{2,1,0:T(1,128)} %reshape.167), calls=%async_computation.2 | async-start | bytes 65536 | tf_op jit(solution)/shard_map/all_to_all | solution.py:68
Sparse Core Ops, SparseCore 0:
  9.5 134.3 all-gather.1
